TPU v7x, 128 devices: a whole 4x4x4 slice. The times are simulated.
128 devices in a mesh: group: 16 (over x, z), mp: 8 (over y, core).
Axes of the slice: x: 4, y: 4, z: 4, core: 2. Of those that a mesh axis runs over, the one named last changes fastest.
Arguments:
- stream: bfloat16 [8192, 3584], P('group', 'mp'), may hold values from -6 to 6
- prenorm_gain: float32 [3584], replicated, may hold values from 0.25 to 12
- query_weight: bfloat16 [3584, 4096], P(None, 'mp'), may hold values from -0.09375 to 0.09375
- key_weight: bfloat16 [3584, 2048], P(None, 'mp'), may hold values from -0.09375 to 0.09375
- value_weight: bfloat16 [3584, 2048], P(None, 'mp'), may hold values from -0.09375 to 0.09375
- output_weight: bfloat16 [4096, 3584], P('mp'), may hold values from -0.09375 to 0.09375
- adapter_down_rows: bfloat16 [64, 16, 3584], P('group', None, 'mp'), may hold values from -0.09375 to 0.09375
- adapter_up_query: bfloat16 [64, 16, 4096], P('group', None, 'mp'), may hold values from -1.5 to 1.5
- request_adapter: int32 [16, 4], replicated, may hold values from 0 to 63
- adapter_row_index: int32 [64], replicated, may hold values from 0 to 63, each once
- request_token_length: int32 [16, 4], replicated, may hold values from 1 to 256, 512 in all within a row
- continues_previous: int32 [16], replicated, may hold values from 0 to 1, as said below
- request_cache_block: int32 [16, 4], replicated, may hold values from 0 to 31, as said below
- cached_length: int32 [16, 4], replicated, may hold values from 1 to 256
- cached_rotated_keys: bfloat16 [32, 256, 2048], P('group', None, 'mp'), may hold values from -6 to 6
- cached_value_rows: bfloat16 [32, 256, 2048], P('group', None, 'mp'), may hold values from -6 to 6
Outputs:
- attn_out: bfloat16 [8192, 3584], P('group', 'mp')
Inputs may be any that keep to these rules, and one draw needn't show every extreme that they name: `continues_previous`: the first group has 0; some group has 1. `request_cache_block`: the owner of block b is group b // 2; blocks may be shared by requests.
All inputs are finite; a program needn't handle non-finite values.
Results may differ from a plain program's by a relative error of at most 0.017.
The roundings to bfloat16 on the way count: a program that leaves them out, or rounds other values in their place, can miss the bound.
Values may be sent and summed in bfloat16 or wider, within the bound.
No kernel may reach another device: no remote copies, remote signals or barrier semaphores. Data moves between devices by JAX's collectives and lax.ppermute only.
A program may use at most 128 MiB of HBM per device.

v0:
```python
import jax
import jax.numpy as jnp
from jax import lax
from jax.sharding import PartitionSpec as P

HEAD_WIDTH = 256
REQS = 4


adapter_scale = 2.0


def shifted(value, axis, steps):
    count = lax.axis_size(axis)
    first, last = (max(0, -steps), min(count, count - steps))
    return lax.ppermute(value, axis, [(source, source + steps) for source in range(first, last)])


def rotate(values, position, head_size):
    count = values.shape[0]
    shaped = values.reshape(count, -1, head_size)
    half = head_size // 2
    freq = 10000.0 ** (-jnp.arange(half, dtype=jnp.float32) / half)
    angle = position[:, None, None] * freq[None, None, :]
    cosine = jnp.cos(angle)
    sine = jnp.sin(angle)
    first = shaped[..., :half]
    second = shaped[..., half:]
    turned = jnp.concatenate(
        [first * cosine - second * sine, second * cosine + first * sine], axis=-1
    )
    return turned.reshape(count, -1)


def layout(lengths, cached, split_flag, prev_len, count):
    ends = jnp.cumsum(lengths)
    starts = ends - lengths
    place = jnp.arange(count, dtype=jnp.int32)
    member = ((place[:, None] >= starts[None, :]) & (place[:, None] < ends[None, :])).astype(
        jnp.int32
    )
    request = jnp.sum(member * jnp.arange(lengths.shape[0], dtype=jnp.int32)[None, :], axis=1)
    offset = place - jnp.sum(member * starts[None, :], axis=1)
    extra = jnp.where(request == 0, split_flag * prev_len, 0)
    position = jnp.sum(member * cached[None, :], axis=1) + extra + offset
    return (member, request, position.astype(jnp.float32))


def attend(
    query_vectors,
    keys,
    values,
    prev_keys,
    prev_values,
    cache_keys,
    cache_values,
    request,
    cached,
    split_flag,
    prev_len,
    head_size,
):
    count = query_vectors.shape[0]
    kv_heads = keys.shape[1] // head_size
    ratio = query_vectors.shape[1] // keys.shape[1]
    block = cache_keys.shape[1]
    slots = cache_keys.shape[0] * block
    every_key = jnp.concatenate([cache_keys.reshape(slots, -1), prev_keys, keys], 0).reshape(
        -1, kv_heads, head_size
    )
    every_value = jnp.concatenate(
        [cache_values.reshape(slots, -1), prev_values, values], 0
    ).reshape(-1, kv_heads, head_size)
    slot_req = jnp.arange(slots, dtype=jnp.int32) // block
    slot_col = jnp.arange(slots, dtype=jnp.int32) % block
    cache_ok = (request[:, None] == slot_req[None, :]) & (
        slot_col[None, :] < cached[slot_req][None, :]
    )
    place = jnp.arange(count, dtype=jnp.int32)
    prev_ok = (split_flag == 1) & (request[:, None] == 0) & (place[None, :] >= count - prev_len)
    own_ok = (request[:, None] == request[None, :]) & (place[None, :] <= place[:, None])
    allowed = jnp.concatenate([cache_ok, prev_ok, own_ok], 1)
    grouped = query_vectors.reshape(count, kv_heads, ratio, head_size)
    scores = jnp.einsum(
        "tkrd,skd->krts", grouped, every_key, preferred_element_type=jnp.float32
    ) * head_size ** (-0.5)
    scores = jnp.where(allowed[None, None], scores, jnp.float32(-1e30))
    top = jnp.max(scores, axis=-1, keepdims=True)
    weights = jnp.exp(scores - top)
    total = jnp.sum(weights, axis=-1)
    numer = jnp.einsum(
        "krts,skd->tkrd",
        weights.astype(jnp.bfloat16),
        every_value,
        preferred_element_type=jnp.float32,
    )
    result = numer / jnp.transpose(total, (2, 0, 1))[..., None]
    return result.reshape(count, -1).astype(jnp.bfloat16)


def on_device(
    stream,
    prenorm_gain,
    query_weight,
    key_weight,
    value_weight,
    output_weight,
    adapter_down_rows,
    adapter_up_query,
    request_adapter,
    adapter_row_index,
    request_token_length,
    continues_previous,
    request_cache_block,
    cached_length,
    cached_rotated_keys,
    cached_value_rows,
):
    count = stream.shape[0]
    width = stream.shape[1]
    group_at = lax.axis_index("group")
    model_at = lax.axis_index("mp")
    whole = lax.all_gather(stream, "mp", axis=1, tiled=True)
    wide = whole.astype(jnp.float32)
    normalized_input = (
        wide * lax.rsqrt(jnp.mean(wide * wide, axis=1, keepdims=True) + 1e-06) * prenorm_gain
    ).astype(jnp.bfloat16)
    normed_part = lax.dynamic_slice_in_dim(normalized_input, model_at * width, width, 1)
    before = jnp.maximum(group_at - 1, 0)
    lengths = request_token_length[group_at]
    cached = cached_length[group_at]
    split_flag = continues_previous[group_at]
    prev_len = request_token_length[before, REQS - 1]
    member, request, position = layout(lengths, cached, split_flag, prev_len, count)
    wanted = adapter_row_index[request_adapter[group_at]]
    pieces = (
        lax.all_gather(adapter_down_rows, "group", axis=0, tiled=True),
        lax.all_gather(adapter_up_query, "group", axis=0, tiled=True),
    )
    stored = jnp.arange(pieces[0].shape[0], dtype=jnp.int32)
    onehot = (wanted[:, None] == stored[None, :]).astype(jnp.bfloat16)
    new_down = jnp.einsum("rj,jkd->rkd", onehot, pieces[0], preferred_element_type=jnp.float32)
    new_up = jnp.einsum("rj,jkd->rkd", onehot, pieces[1], preferred_element_type=jnp.float32)
    chosen_down = new_down.astype(jnp.bfloat16)
    chosen_up = new_up.astype(jnp.bfloat16)
    rank_index = adapter_down_rows.shape[1]
    partial_low = jnp.einsum(
        "td,rkd->trk", normed_part, chosen_down, preferred_element_type=jnp.float32
    ).reshape(count, REQS * rank_index)
    low = lax.psum(partial_low, "mp").astype(jnp.bfloat16)
    own_columns = jnp.repeat(member, rank_index, axis=1).astype(jnp.bfloat16)
    query_update = jnp.dot(
        low * own_columns,
        chosen_up.reshape(REQS * rank_index, -1),
        preferred_element_type=jnp.float32,
    )
    query_vectors = (
        jnp.dot(normalized_input, query_weight, preferred_element_type=jnp.float32)
        + adapter_scale * query_update
    )
    query_vectors = rotate(query_vectors, position, HEAD_WIDTH).astype(jnp.bfloat16)
    keys = rotate(
        jnp.dot(normalized_input, key_weight, preferred_element_type=jnp.float32),
        position,
        HEAD_WIDTH,
    ).astype(jnp.bfloat16)
    values = jnp.dot(normalized_input, value_weight, preferred_element_type=jnp.float32).astype(
        jnp.bfloat16
    )
    prev_keys, prev_values = shifted((keys, values), "group", 1)
    blocks = request_cache_block[group_at]
    pieces = (
        lax.all_gather(cached_rotated_keys, "group", axis=0, tiled=True),
        lax.all_gather(cached_value_rows, "group", axis=0, tiled=True),
    )
    stored = jnp.arange(pieces[0].shape[0], dtype=jnp.int32)
    onehot = (blocks[:, None] == stored[None, :]).astype(jnp.bfloat16)
    new_keys = jnp.einsum("rj,jcd->rcd", onehot, pieces[0], preferred_element_type=jnp.float32)
    new_values = jnp.einsum("rj,jcd->rcd", onehot, pieces[1], preferred_element_type=jnp.float32)
    cache_keys = new_keys.astype(jnp.bfloat16)
    cache_values = new_values.astype(jnp.bfloat16)
    attended = attend(
        query_vectors,
        keys,
        values,
        prev_keys,
        prev_values,
        cache_keys,
        cache_values,
        request,
        cached,
        split_flag,
        prev_len,
        HEAD_WIDTH,
    )
    partial_out = jnp.dot(attended, output_weight, preferred_element_type=jnp.float32)
    return lax.psum_scatter(partial_out.astype(jnp.bfloat16), "mp", scatter_dimension=1, tiled=True)


def solution(mesh):
    placed = (
        P("group", "mp"),
        P(),
        P(None, "mp"),
        P(None, "mp"),
        P(None, "mp"),
        P("mp", None),
        P("group", None, "mp"),
        P("group", None, "mp"),
        P(),
        P(),
        P(),
        P(),
        P(),
        P(),
        P("group", None, "mp"),
        P("group", None, "mp"),
    )
    return jax.shard_map(
        on_device, mesh=mesh, in_specs=placed, out_specs=P("group", "mp"), check_vma=False
    )
```

profile of v0, /device:TPU:0, one launch (start us, length us, event | category | flops | bytes accessed | tf_op | source)
XLA Modules:
  0.0 254.0 jit_solution(16617972660007501374)
XLA Ops:
  6.5 0.7 all-gather.11.cloned.1.call-update
  7.3 0.0 all-gather.7.cloned.1.call-start
  7.3 0.7 all-gather.7.cloned.1.call-update
  8.0 0.0 all-gather.5.cloned.1.call-start
  8.1 0.7 all-gather.5.cloned.1.call-update
  8.7 0.0 all-gather.9.cloned.1.call-start
  8.8 0.5 all-gather.9.cloned.1.call-update
  9.3 0.0 reduce-scatter.2.cloned.1.call-start
  9.4 1.3 constant_dynamic-slice_fusion.2
  10.7 0.9 dynamic-slice_reduce_fusion
  11.6 0.1 copy.61
  11.7 0.2 reduce-window.4
  11.9 0.9 fusion.79
  12.8 0.6 fusion.81
  13.4 26.9 %all_gather.18 = bf16[64,16,448]{2,1,0:T(8,128)(2,1)S(1)} all-gather(bf16[4,16,448]{2,1,0:T(8,128)(2,1)} %param.22), channel_id=1, replica_groups=mesh['group'=16,'mp'=8] {'group'}, dimensions={0}, use_global_device_ids=true | all-gather | bytes 974848 | tf_op jit(solution)/shard_map/all_gather | solution.py:137
  40.9 2.6 %compare_select_fusion.1 = s32[1024,1]{0,1:T(1,128)S(1)} fusion(s32[]{:T(128)} %bitcast.7, s32[]{:T(128)} %bitcast.8, s32[]{:T(128)} %bitcast.10, s32[]{:T(128)} %bitcast.9), kind=kLoop, calls=%fused_computation.71 | loop fusion | flops 17408 | bytes 4112 | tf_op jit(solution)/shard_map/gather | solution.py:77
  43.5 1.2 dynamic_slice.24
  46.8 0.9 dynamic-slice_reduce_fusion.1
  47.6 1.3 gather_fusion
  48.9 0.1 select_reduce_fusion.2
  49.0 0.1 convert_convert_fusion
  49.1 0.2 broadcast_and_fusion
  49.3 0.2 fusion.35
  49.5 1.8 multiply_cosine_fusion
  51.4 0.8 compare_and_fusion
  52.2 1.2 convolution_convert_fusion.3
  53.4 0.4 pad_add_fusion
  53.8 1.2 all-gather.11.cloned.1.call-done
  54.9 2.4 convolution_convert_fusion.2
  57.4 28.5 %all-gather.7.cloned.1.call-done = bf16[512,3584]{0,1:T(8,128)(2,1)} async-done(((bf16[512,448]{0,1:T(8,128)(2,1)}), bf16[512,3584]{0,1:T(8,128)(2,1)}) %all-gather.7.cloned.1.call-update) | async-done | bytes 3670032 | tf_op jit(solution)/shard_map/all_gather | solution.py:123
  85.8 3.0 %fusion.2 = f32[512]{0:T(512)S(1)} fusion(bf16[512,3584]{0,1:T(8,128)(2,1)} %all-gather.7.cloned.1.call-done), kind=kLoop, calls=%fused_computation.7 | loop fusion | flops 5504512 | bytes 3672064 | tf_op jit(solution)/shard_map/reduce_sum | solution.py:126
  88.9 0.1 copy-done.1
  89.0 1.6 fusion.4
  90.6 1.8 copy-done.2
  92.4 1.9 convolution_convert_fusion.1
  94.3 1.8 copy.47
  96.1 4.2 %collective-permute-start = (bf16[512,256]{1,0:T(8,128)(2,1)}, bf16[512,256]{1,0:T(8,128)(2,1)}, u32[]{:S(2)}, u32[]{:S(2)}) collective-permute-start(bf16[512,256]{1,0:T(8,128)(2,1)} %convolution_convert_fusion.1), channel_id=1, source_target_pairs={{0,8},{8,16},{16,24},{24,32},{32,40},{40,48},{48,56},{56,64},{64,7... | collective-permute-start | bytes 786440 | tf_op jit(solution)/shard_map/ppermute | solution.py:16
  100.2 3.8 %convolution_bitcast_fusion = f32[512,1,256]{0,2,1:T(8,128)S(1)} fusion(bf16[512,3584]{0,1:T(8,128)(2,1)} %copy-done.2, bf16[3584,256]{1,0:T(8,128)(2,1)} %param.19), kind=kOutput, calls=%fused_computation.26 | convolution fusion | flops 939524096 | bytes 6029312 | tf_op jit(solution)/shard_map/dot_general | solution.py:163
  104.0 1.2 fusion.49
  105.2 0.7 maximum_bitcast_fusion.6
  105.9 1.8 copy.52
  107.7 3.4 %collective-permute-start.1 = (bf16[512,256]{0,1:T(8,128)(2,1)}, bf16[512,256]{0,1:T(8,128)(2,1)}, u32[]{:S(2)}, u32[]{:S(2)}) collective-permute-start(bf16[512,256]{0,1:T(8,128)(2,1)} %maximum_bitcast_fusion.6), channel_id=1, source_target_pairs={{0,8},{8,16},{16,24},{24,32},{32,40},{40,48},{48,56},{56,64},{64,7... | collective-permute-start | bytes 786440 | tf_op jit(solution)/shard_map/ppermute | solution.py:16
  111.1 1.2 fusion.41
  112.3 26.0 %all-reduce.1 = bf16[512,64]{0,1:T(8,128)(2,1)S(1)} all-reduce(f32[512,64]{0,1:T(8,128)S(1)} %bitcast.101), channel_id=1, replica_groups=mesh['group'=16,'mp'=8] {'mp'}, use_global_device_ids=true, to_apply=%region_5.6 | all-reduce | flops 32768 | bytes 196608 | tf_op jit(solution)/shard_map/psum | solution.py:150
  138.4 5.3 %fusion.82 = f32[512,512]{0,1:T(8,128)S(1)} fusion(bf16[512,3584]{0,1:T(8,128)(2,1)} %copy-done.2, bf16[3584,512]{1,0:T(8,128)(2,1)} %param.18), kind=kOutput, calls=%fused_computation.129 | convolution fusion | flops 1879048192 | bytes 8388608 | tf_op jit(solution)/shard_map/dot_general | solution.py:158
  143.7 0.3 fusion.17
  144.0 1.1 fusion.80
  145.1 1.2 copy.63
  146.4 2.1 copy.62
  148.5 2.2 subtract_convert_fusion
  150.6 1.8 copy.46
  152.5 1.8 copy.51
  154.3 4.6 %fusion.18 = bf16[4,256,256]{2,0,1:T(4,128)(2,1)S(1)} fusion(bf16[32,256,256]{2,1,0:T(8,128)(2,1)} %all-gather.5.cloned.1.call-done, s32[4]{0:T(128)S(1)} %dynamic-slice_reduce_fusion.1), kind=kOutput, calls=%fused_computation.24 | convolution fusion | flops 17039488 | bytes 4718608 | tf_op jit(solution)/shard_map/rj,jcd->rcd/dot_general | solution.py:179
  158.9 0.1 copy.44
  159.0 1.0 copy.45
  160.0 35.3 %all-gather.9.cloned.1.call-done = bf16[32,256,256]{2,1,0:T(8,128)(2,1)} async-done(((bf16[2,256,256]{2,1,0:T(8,128)(2,1)}), bf16[32,256,256]{2,1,0:T(8,128)(2,1)}) %all-gather.9.cloned.1.call-update) | async-done | bytes 4194320 | tf_op jit(solution)/shard_map/all_gather | solution.py:173
  195.3 4.7 %fusion.21 = bf16[4,256,256]{2,0,1:T(4,128)(2,1)S(1)} fusion(bf16[32,256,256]{2,1,0:T(8,128)(2,1)} %all-gather.9.cloned.1.call-done, s32[4]{0:T(128)S(1)} %dynamic-slice_reduce_fusion.1), kind=kOutput, calls=%fused_computation.25 | convolution fusion | flops 17039488 | bytes 4718608 | tf_op jit(solution)/shard_map/rj,jcd->rcd/dot_general | solution.py:178
  200.0 0.1 copy.50
  200.1 1.8 fusion.5
  201.9 2.2 fusion
  204.2 2.8 %divide_convert_fusion = bf16[512,1,2,256]{0,3,2,1:T(8,128)(2,1)S(1)} fusion(f32[2048,512,2]{1,0,2:T(8,128)S(1)} %get-tuple-element.25, f32[2,512]{1,0:T(2,128)S(1)} %get-tuple-element.24, pred[512,2048]{0,1:T(8,128)(4,1)S(1)} %pad_add_fusion, bf16[512,256]{0,1:T(8,128)(2,1)S(1)} %copy-done.4, bf16[512,256]{0,1:T(8,128)(2,1)S(1)} %copy-done.6, ...), kind=kOutput, calls=%fused_computation.43 | convolution fusion | flops 1085800448 | bytes 11018240 | tf_op jit(solution)/shard_map/krts,skd->tkrd/dot_general | solution.py:91
  207.0 3.9 %convolution_convert_fusion = bf16[512,3584]{0,1:T(8,128)(2,1)} fusion(bf16[512,512]{0,1:T(8,128)(2,1)S(1)} %bitcast.107, bf16[512,3584]{1,0:T(8,128)(2,1)S(1)} %copy-done.11), kind=kOutput, calls=%fused_computation.11 | convolution fusion | flops 1880883200 | bytes 7864320 | tf_op jit(solution)/shard_map/dot_general | solution.py:196
  210.9 0.0 reduce-scatter.2.cloned.1.call-update
  210.9 36.5 %reduce-scatter.2.cloned.1.call-done = bf16[512,448]{0,1:T(8,128)(2,1)} async-done(((bf16[512,3584]{0,1:T(8,128)(2,1)}), bf16[512,448]{0,1:T(8,128)(2,1)}) %reduce-scatter.2.cloned.1.call-update) | async-done | bytes 458768 | tf_op jit(solution)/shard_map/reduce_scatter | solution.py:197
  (38 shorter events, 0.2 us)
Async XLA Ops:
  6.5 85.8 %copy-start = (bf16[3584,256]{1,0:T(8,128)(2,1)S(1)}, bf16[3584,256]{1,0:T(8,128)(2,1)}, u32[]{:S(2)}) copy-start(bf16[3584,256]{1,0:T(8,128)(2,1)} %param.20) | copy-start | bytes 5505028
  6.5 48.4 %all-gather.11.cloned.1.call-start = ((), (), s32[]{:S(2)}) async-start(), calls=%async_computation.4 | async-start | bytes 1114112 | tf_op jit(solution)/shard_map/all_gather | solution.py:138
  7.3 78.6 %all-gather.7.cloned.1.call-start = ((), (), s32[]{:S(2)}) async-start(), calls=%async_computation.2 | async-start | bytes 4128768 | tf_op jit(solution)/shard_map/all_gather | solution.py:123
  8.0 146.3 %all-gather.5.cloned.1.call-start = ((), (), s32[]{:S(2)}) async-start(), calls=%async_computation.1 | async-start | bytes 4456448 | tf_op jit(solution)/shard_map/all_gather | solution.py:174
  8.7 186.5 %all-gather.9.cloned.1.call-start = ((), (), s32[]{:S(2)}) async-start(), calls=%async_computation.3 | async-start | bytes 4456448 | tf_op jit(solution)/shard_map/all_gather | solution.py:173
  9.3 238.1 %reduce-scatter.2.cloned.1.call-start = ((), (), s32[]{:S(2)}) async-start(), calls=%async_computation.5 | async-start | bytes 4128768 | tf_op jit(solution)/shard_map/reduce_scatter | solution.py:197
  53.4 35.5 %copy-start.10 = (f32[3584]{0:T(1024)S(1)}, f32[3584]{0:T(1024)}, u32[]{:S(2)}) copy-start(f32[3584]{0:T(1024)} %param.17) | copy-start | bytes 43012
  85.8 3.1 %copy-start.1 = (bf16[512,3584]{0,1:T(8,128)(2,1)S(1)}, bf16[512,3584]{0,1:T(8,128)(2,1)}, u32[]{:S(2)}) copy-start(bf16[512,3584]{0,1:T(8,128)(2,1)} %all-gather.7.cloned.1.call-done) | copy-start | bytes 11010052
  90.5 1.8 copy-start.2
  96.1 54.6 %collective-permute-start = (bf16[512,256]{1,0:T(8,128)(2,1)}, bf16[512,256]{1,0:T(8,128)(2,1)}, u32[]{:S(2)}, u32[]{:S(2)}) collective-permute-start(bf16[512,256]{1,0:T(8,128)(2,1)} %convolution_convert_fusion.1), channel_id=1, source_target_pairs={{0,8},{8,16},{16,24},{24,32},{32,40},{40,48},{48,56},{56,64},{64,7... | collective-permute-start | bytes 786440 | tf_op jit(solution)/shard_map/ppermute | solution.py:16
  107.7 44.8 %collective-permute-start.1 = (bf16[512,256]{0,1:T(8,128)(2,1)}, bf16[512,256]{0,1:T(8,128)(2,1)}, u32[]{:S(2)}, u32[]{:S(2)}) collective-permute-start(bf16[512,256]{0,1:T(8,128)(2,1)} %maximum_bitcast_fusion.6), channel_id=1, source_target_pairs={{0,8},{8,16},{16,24},{24,32},{32,40},{40,48},{48,56},{56,64},{64,7... | collective-permute-start | bytes 786440 | tf_op jit(solution)/shard_map/ppermute | solution.py:16
  160.0 40.1 %copy-start.5 = (bf16[512,256]{1,0:T(8,128)(2,1)S(1)}, bf16[512,256]{1,0:T(8,128)(2,1)}, u32[]{:S(2)}) copy-start(bf16[512,256]{1,0:T(8,128)(2,1)} %copy.52) | copy-start | bytes 786436
  160.0 40.1 %copy-start.7 = (bf16[512,256]{1,0:T(8,128)(2,1)S(1)}, bf16[512,256]{1,0:T(8,128)(2,1)}, u32[]{:S(2)}) copy-start(bf16[512,256]{1,0:T(8,128)(2,1)} %copy.51) | copy-start | bytes 786436
  195.3 4.8 %copy-start.8 = (bf16[512,2,128]{2,0,1:T(8,128)(2,1)S(1)}, bf16[512,2,128]{2,0,1:T(8,128)(2,1)}, u32[]{:S(2)}) copy-start(bf16[512,2,128]{2,0,1:T(8,128)(2,1)} %get-tuple-element.12) | copy-start | bytes 786436
  195.3 4.8 %copy-start.9 = (bf16[512,2,128]{2,0,1:T(8,128)(2,1)S(1)}, bf16[512,2,128]{2,0,1:T(8,128)(2,1)}, u32[]{:S(2)}) copy-start(bf16[512,2,128]{2,0,1:T(8,128)(2,1)} %get-tuple-element.13) | copy-start | bytes 786436
  201.9 2.2 copy-start.3
  201.9 2.2 copy-start.4
  201.9 2.2 copy-start.6
  204.2 2.8 %copy-start.11 = (bf16[512,3584]{1,0:T(8,128)(2,1)S(1)}, bf16[512,3584]{1,0:T(8,128)(2,1)}, u32[]{:S(2)}) copy-start(bf16[512,3584]{1,0:T(8,128)(2,1)} %param.21) | copy-start | bytes 11010052
Sparse Core Ops, SparseCore 0:
  9.5 45.3 all-gather.10
  56.6 29.1 all-gather.6
  88.0 53.9 all-gather.4
  144.0 51.2 all-gather.8
  211.0 36.3 reduce-scatter.1
where the time goes:
time: 255 us; the launch traced here: 254 us
  waiting for transfers between devices  104 us (41%)
  blocking collectives  52.9 us (21%)
  matrix products  33.9 us (13%)
  local copies, waits for them, and re-layouts  21.9 us (9%)
  other arithmetic  17.3 us (7%)
  between operations  16.1 us (6%)
  starting transfers between devices  7.77 us (3%)
    reduce_scatter x1, waiting for transfers between devices, on_device(): lax.psum_scatter(partial_out.astype(jnp.bfloat16), 'mp', scatter_dimensio...  36.5 us
    all_gather x1, waiting for transfers between devices, on_device(): lax.all_gather(cached_rotated_keys, 'group', axis=0, tiled=True)  35.3 us
    all_gather x1, waiting for transfers between devices, on_device(): whole = lax.all_gather(stream, 'mp', axis=1, tiled=True)  28.5 us
    all_gather x1, blocking collectives, on_device(): lax.all_gather(adapter_down_rows, 'group', axis=0, tiled=True)  26.9 us
    psum x1, blocking collectives, on_device(): low = lax.psum(partial_low, 'mp').astype(jnp.bfloat16)  26 us
    ppermute x2, starting transfers between devices, shifted(): lax.ppermute(value, axis, [(source, source + steps) for source in range(f...  7.62 us
    unnamed x27, local copies, waits for them, and re-layouts  5.37 us
    dot_general x1, matrix products, on_device(): jnp.dot(normalized_input, query_weight, preferred_element_type=jnp.float32)  5.26 us
  transfers between devices with their start and end apart: 7, of which 4 were waited for; matrix products, arithmetic and copies ran while one was open for 22% of the time, Pallas kernels for 0%

commit v1 on v0

--- a/solution.py
+++ b/solution.py
@@ -1,7 +1,7 @@
 import jax
 import jax.numpy as jnp
 from jax import lax
-from jax.sharding import PartitionSpec as P
+from jax.sharding import Mesh, PartitionSpec as P
 
 HEAD_WIDTH = 256
 REQS = 4
@@ -98,6 +98,63 @@
     return result.reshape(count, -1).astype(jnp.bfloat16)
 
 
+SIDE = 4
+
+
+def ring_gather(value, axis):
+    held = [value]
+    for step in range(1, SIDE):
+        held.append(lax.ppermute(value, axis, [(i, (i + step) % SIDE) for i in range(SIDE)]))
+    return jnp.stack(held)
+
+
+def group_of(first, a_coord, b_coord):
+    return b_coord * SIDE + a_coord if first == "gz" else a_coord * SIDE + b_coord
+
+
+def route(local, wanted, first, second):
+    per_owner = local.shape[0]
+    coords = {"gx": lax.axis_index("gx"), "gz": lax.axis_index("gz")}
+    own_a, own_b = coords[first], coords[second]
+    owner = wanted // per_owner
+    owner_coords = {"gx": owner // SIDE, "gz": owner % SIDE}
+    owner_a, owner_b = owner_coords[first], owner_coords[second]
+    part = wanted % per_owner
+    held = ring_gather(local, first).reshape(SIDE * per_owner, *local.shape[1:])
+
+    def pick(requester_b):
+        asker = group_of(first, own_a, requester_b)
+        shift = (own_a - owner_a[asker]) % SIDE
+        return held[shift * per_owner + part[asker]]
+
+    received = [pick(own_b)]
+    for step in range(1, SIDE):
+        payload = pick((own_b + step) % SIDE)
+        received.append(
+            lax.ppermute(payload, second, [(i, (i + step) % SIDE) for i in range(SIDE)])
+        )
+    stacked = jnp.stack(received)
+    me = group_of(first, own_a, own_b)
+    came_from = (own_b - owner_b[me]) % SIDE
+    return stacked[came_from, jnp.arange(wanted.shape[1])]
+
+
+def gather_model(value, axis):
+    count = 8
+    model_at = lax.axis_index(("my", "mc"))
+    held = [value]
+    for step in range(1, count):
+        held.append(
+            lax.ppermute(value, ("my", "mc"), [(i, (i + step) % count) for i in range(count)])
+        )
+    held = jnp.stack(held)
+    ordered = held[(model_at - jnp.arange(count)) % count]
+    moved = jnp.moveaxis(ordered, 0, axis)
+    shape = list(value.shape)
+    shape[axis] = shape[axis] * count
+    return moved.reshape(shape)
+
+
 def on_device(
     stream,
     prenorm_gain,
@@ -117,37 +174,32 @@
     cached_value_rows,
 ):
     count = stream.shape[0]
-    width = stream.shape[1]
-    group_at = lax.axis_index("group")
-    model_at = lax.axis_index("mp")
-    whole = lax.all_gather(stream, "mp", axis=1, tiled=True)
+    group_at = lax.axis_index(("gx", "gz"))
+    wanted = adapter_row_index[request_adapter]
+    down_width = adapter_down_rows.shape[2]
+    adapters = jnp.concatenate([adapter_down_rows, adapter_up_query], axis=2)
+    chosen = route(adapters, wanted, "gz", "gx")
+    chosen_down = chosen[:, :, :down_width]
+    chosen_up = chosen[:, :, down_width:]
+    cache_keys = route(cached_rotated_keys, request_cache_block, "gz", "gx")
+    cache_values = route(cached_value_rows, request_cache_block, "gx", "gz")
+    full_down = gather_model(chosen_down, 2)
+
+    whole = lax.all_gather(stream, ("my", "mc"), axis=1, tiled=True)
     wide = whole.astype(jnp.float32)
     normalized_input = (
         wide * lax.rsqrt(jnp.mean(wide * wide, axis=1, keepdims=True) + 1e-06) * prenorm_gain
     ).astype(jnp.bfloat16)
-    normed_part = lax.dynamic_slice_in_dim(normalized_input, model_at * width, width, 1)
     before = jnp.maximum(group_at - 1, 0)
     lengths = request_token_length[group_at]
     cached = cached_length[group_at]
     split_flag = continues_previous[group_at]
     prev_len = request_token_length[before, REQS - 1]
     member, request, position = layout(lengths, cached, split_flag, prev_len, count)
-    wanted = adapter_row_index[request_adapter[group_at]]
-    pieces = (
-        lax.all_gather(adapter_down_rows, "group", axis=0, tiled=True),
-        lax.all_gather(adapter_up_query, "group", axis=0, tiled=True),
-    )
-    stored = jnp.arange(pieces[0].shape[0], dtype=jnp.int32)
-    onehot = (wanted[:, None] == stored[None, :]).astype(jnp.bfloat16)
-    new_down = jnp.einsum("rj,jkd->rkd", onehot, pieces[0], preferred_element_type=jnp.float32)
-    new_up = jnp.einsum("rj,jkd->rkd", onehot, pieces[1], preferred_element_type=jnp.float32)
-    chosen_down = new_down.astype(jnp.bfloat16)
-    chosen_up = new_up.astype(jnp.bfloat16)
     rank_index = adapter_down_rows.shape[1]
-    partial_low = jnp.einsum(
-        "td,rkd->trk", normed_part, chosen_down, preferred_element_type=jnp.float32
-    ).reshape(count, REQS * rank_index)
-    low = lax.psum(partial_low, "mp").astype(jnp.bfloat16)
+    low = jnp.einsum(
+        "td,rkd->trk", normalized_input, full_down, preferred_element_type=jnp.float32
+    ).reshape(count, REQS * rank_index).astype(jnp.bfloat16)
     own_columns = jnp.repeat(member, rank_index, axis=1).astype(jnp.bfloat16)
     query_update = jnp.dot(
         low * own_columns,
@@ -167,18 +219,7 @@
     values = jnp.dot(normalized_input, value_weight, preferred_element_type=jnp.float32).astype(
         jnp.bfloat16
     )
-    prev_keys, prev_values = shifted((keys, values), "group", 1)
-    blocks = request_cache_block[group_at]
-    pieces = (
-        lax.all_gather(cached_rotated_keys, "group", axis=0, tiled=True),
-        lax.all_gather(cached_value_rows, "group", axis=0, tiled=True),
-    )
-    stored = jnp.arange(pieces[0].shape[0], dtype=jnp.int32)
-    onehot = (blocks[:, None] == stored[None, :]).astype(jnp.bfloat16)
-    new_keys = jnp.einsum("rj,jcd->rcd", onehot, pieces[0], preferred_element_type=jnp.float32)
-    new_values = jnp.einsum("rj,jcd->rcd", onehot, pieces[1], preferred_element_type=jnp.float32)
-    cache_keys = new_keys.astype(jnp.bfloat16)
-    cache_values = new_values.astype(jnp.bfloat16)
+    prev_keys, prev_values = shifted((keys, values), ("gx", "gz"), 1)
     attended = attend(
         query_vectors,
         keys,
@@ -194,28 +235,33 @@
         HEAD_WIDTH,
     )
     partial_out = jnp.dot(attended, output_weight, preferred_element_type=jnp.float32)
-    return lax.psum_scatter(partial_out.astype(jnp.bfloat16), "mp", scatter_dimension=1, tiled=True)
+    return lax.psum_scatter(
+        partial_out.astype(jnp.bfloat16), ("my", "mc"), scatter_dimension=1, tiled=True
+    )
 
 
 def solution(mesh):
+    split = Mesh(mesh.devices.reshape(SIDE, SIDE, 4, 2), ("gx", "gz", "my", "mc"))
+    groups = ("gx", "gz")
+    model = ("my", "mc")
     placed = (
-        P("group", "mp"),
-        P(),
-        P(None, "mp"),
-        P(None, "mp"),
-        P(None, "mp"),
-        P("mp", None),
-        P("group", None, "mp"),
-        P("group", None, "mp"),
-        P(),
-        P(),
-        P(),
-        P(),
-        P(),
-        P(),
-        P("group", None, "mp"),
-        P("group", None, "mp"),
+        P(groups, model),
+        P(),
+        P(None, model),
+        P(None, model),
+        P(None, model),
+        P(model, None),
+        P(groups, None, model),
+        P(groups, None, model),
+        P(),
+        P(),
+        P(),
+        P(),
+        P(),
+        P(),
+        P(groups, None, model),
+        P(groups, None, model),
     )
     return jax.shard_map(
-        on_device, mesh=mesh, in_specs=placed, out_specs=P("group", "mp"), check_vma=False
-    )
+        on_device, mesh=split, in_specs=placed, out_specs=P(groups, model), check_vma=False
+    )

time: 255 us -> 249 us (0.976)
  blocking collectives: 52.9 us -> 0 us
  waiting for transfers between devices: 104 us -> 57.1 us
  starting transfers between devices: 7.77 us -> 44.6 us
  local copies, waits for them, and re-layouts: 21.9 us -> 58.3 us
  other arithmetic: 17.3 us -> 42.4 us
  matrix products: 33.9 us -> 28.5 us
    all_gather x4 -> x1, waiting for transfers between devices: 64.9 us -> 0.01 us  [on_device(): whole = lax.all_gather(stream, ('my', 'mc'), axis=1, tiled=True)]
    ppermute x0 -> x25, starting transfers between devices: none -> 38.6 us  [the longest x9 15.8 us: route(): lax.ppermute(payload, second, [(i, (i + step) % SIDE) for i in range(SIDE)])]
    all_gather x1 -> x0, blocking collectives: 26.9 us -> none  [on_device(): lax.all_gather(adapter_down_rows, 'group', axis=0, tiled=True)]
    gather x1 -> x18, local copies, waits for them, and re-layouts: 1.29 us -> 27.9 us  [the longest x12 19.5 us: pick(): return held[shift * per_owner + part[asker]]]
    psum x1 -> x0, blocking collectives: 26 us -> none  [on_device(): low = lax.psum(partial_low, 'mp').astype(jnp.bfloat16)]
    ppermute x0 -> x25, waiting for transfers between devices: none -> 20.4 us  [the longest x9 15.2 us: route(): lax.ppermute(payload, second, [(i, (i + step) % SIDE) for i in range(SIDE)])]
    dot_general x5 -> x0, matrix products: 14.2 us -> none  [the longest x1 4.69 us: on_device(): jnp.einsum('rj,jcd->rcd', onehot, pieces[0], preferred_element_type=jnp.f...]
    another operation x3 -> x10, other arithmetic: 3.52 us -> 16.2 us  [the longest x3 7.18 us: route(): stacked = jnp.stack(received)]
  transfers between devices with their start and end apart: 7 -> 29, of which waited for: 4 -> 6; matrix products, arithmetic and copies ran while one was open for 22% -> 42% of each run, Pallas kernels for 0% -> 0%
where the time goes in v1:
time: 249 us; the launch traced here: 248 us
  local copies, waits for them, and re-layouts  58.3 us (23%)
  waiting for transfers between devices  57.1 us (23%)
  starting transfers between devices  44.6 us (18%)
  other arithmetic  42.4 us (17%)
  matrix products  28.5 us (11%)
  between operations  16.5 us (7%)
    reduce_scatter x1, waiting for transfers between devices, on_device(): lax.psum_scatter(partial_out.astype(jnp.bfloat16), ('my', 'mc'), scatter_...  36.7 us
    gather x12, local copies, waits for them, and re-layouts, pick(): return held[shift * per_owner + part[asker]]  19.5 us
    unnamed x60, local copies, waits for them, and re-layouts  17.5 us
    ppermute x9, starting transfers between devices, route(): lax.ppermute(payload, second, [(i, (i + step) % SIDE) for i in range(SIDE)])  15.8 us
    ppermute x9, waiting for transfers between devices, route(): lax.ppermute(payload, second, [(i, (i + step) % SIDE) for i in range(SIDE)])  15.2 us
    ppermute x9, starting transfers between devices, ring_gather(): lax.ppermute(value, axis, [(i, (i + step) % SIDE) for i in range(SIDE)])  14.4 us
    ppermute x7, starting transfers between devices, gather_model(): lax.ppermute(value, ('my', 'mc'), [(i, (i + step) % count) for i in range...  8.47 us
    another operation x3, other arithmetic, route(): stacked = jnp.stack(received)  7.18 us
  transfers between devices with their start and end apart: 29, of which 6 were waited for; matrix products, arithmetic and copies ran while one was open for 42% of the time, Pallas kernels for 0%

profile of v1, /device:TPU:0, one launch (start us, length us, event | category | flops | bytes accessed | tf_op | source)
XLA Modules:
  0.0 247.6 jit_solution(3504332139167944642)
XLA Ops:
  7.7 4.0 %collective-permute-start.15 = (bf16[4,16,960]{2,1,0:T(8,128)(2,1)S(1)}, bf16[4,16,960]{2,1,0:T(8,128)(2,1)S(1)}, u32[]{:S(2)}, u32[]{:S(2)}) collective-permute-start(bf16[4,16,960]{2,1,0:T(8,128)(2,1)S(1)} %get-tuple-element.26), channel_id=1, source_target_pairs={{0,16},{8,24},{16,0},{24,8},{1,17},{9,25},{17,1},{25,9},{2,18},{10... | collective-permute-start | bytes 368648 | tf_op jit(solution)/shard_map/ppermute | solution.py:107
  12.7 2.2 collective-permute-start.16
  14.9 3.2 %collective-permute-start.9 = (bf16[2,256,256]{2,1,0:T(8,128)(2,1)}, bf16[2,256,256]{2,1,0:T(8,128)(2,1)}, u32[]{:S(2)}, u32[]{:S(2)}) collective-permute-start(bf16[2,256,256]{2,1,0:T(8,128)(2,1)} %param.30), channel_id=1, source_target_pairs={{0,24},{8,0},{16,8},{24,16},{1,25},{9,1},{17,9},{25,17},{2,26},{10... | collective-permute-start | bytes 786440 | tf_op jit(solution)/shard_map/ppermute | solution.py:107
  34.0 2.4 compare_select_fusion.2
  37.5 1.8 multiply_cosine_fusion
  40.2 1.4 pad_add_fusion
  45.8 1.3 gather_fusion.12
  47.2 1.5 collective-permute-start.17
  48.7 2.7 %collective-permute-start.18 = (bf16[4,16,960]{2,1,0:T(8,128)(2,1)S(1)}, bf16[4,16,960]{2,1,0:T(8,128)(2,1)}, u32[]{:S(2)}, u32[]{:S(2)}) collective-permute-start(bf16[4,16,960]{2,1,0:T(8,128)(2,1)S(1)} %gather_fusion.13), channel_id=1, source_target_pairs={{0,64},{32,96},{64,0},{96,32},{1,65},{33,97},{65,1},{97,33},{2,66}... | collective-permute-start | bytes 368648 | tf_op jit(solution)/shard_map/ppermute | solution.py:134
  51.4 1.4 collective-permute-start.19
  52.8 1.3 fusion.151
  56.9 2.7 %collective-permute-start.2 = (bf16[2,256,256]{2,1,0:T(8,128)(2,1)S(1)}, bf16[2,256,256]{2,1,0:T(8,128)(2,1)}, u32[]{:S(2)}, u32[]{:S(2)}) collective-permute-start(bf16[2,256,256]{2,1,0:T(8,128)(2,1)S(1)} %copy-done.10), channel_id=1, source_target_pairs={{0,96},{32,0},{64,32},{96,64},{1,97},{33,1},{65,33},{97,65},{2,98}... | collective-permute-start | bytes 786440 | tf_op jit(solution)/shard_map/ppermute | solution.py:107
  62.6 3.0 %collective-permute-start.25 = (bf16[4,16,448]{2,1,0:T(8,128)(2,1)S(1)}, bf16[4,16,448]{2,1,0:T(8,128)(2,1)}, u32[]{:S(2)}, u32[]{:S(2)}) collective-permute-start(bf16[4,16,448]{2,1,0:T(8,128)(2,1)S(1)} %slice.70), channel_id=1, source_target_pairs={{0,6},{1,7},{2,0},{3,1},{4,2},{5,3},{6,4},{7,5},{8,14},{9,15},{10,... | collective-permute-start | bytes 172040 | tf_op jit(solution)/shard_map/ppermute | solution.py:148
  65.7 1.2 pad_maximum_fusion.3
  66.9 2.7 %collective-permute-done = bf16[2,256,256]{2,1,0:T(8,128)(2,1)} collective-permute-done((bf16[2,256,256]{2,1,0:T(8,128)(2,1)S(1)}, bf16[2,256,256]{2,1,0:T(8,128)(2,1)}, u32[]{:S(2)}, u32[]{:S(2)}) %collective-permute-start) | collective-permute-done | bytes 262176 | tf_op jit(solution)/shard_map/ppermute | solution.py:107
  69.6 3.2 %collective-permute-start.23 = (bf16[4,16,448]{2,1,0:T(8,128)(2,1)S(1)}, bf16[4,16,448]{2,1,0:T(8,128)(2,1)}, u32[]{:S(2)}, u32[]{:S(2)}) collective-permute-start(bf16[4,16,448]{2,1,0:T(8,128)(2,1)S(1)} %slice.70), channel_id=1, source_target_pairs={{0,4},{1,5},{2,6},{3,7},{4,0},{5,1},{6,2},{7,3},{8,12},{9,13},{10,... | collective-permute-start | bytes 172040 | tf_op jit(solution)/shard_map/ppermute | solution.py:148
  73.3 2.1 pad_maximum_fusion.2
  75.4 2.8 %gather_fusion.3 = bf16[4,256,256]{2,1,0:T(8,128)(2,1)} fusion(bf16[8,256,256]{2,1,0:T(8,128)(2,1)} %bitcast.304, s32[1024]{0:T(1024)} %pad_clamp_fusion.10), kind=kCustom, calls=%fused_computation.3 | custom fusion | bytes 1048592 | tf_op jit(solution)/shard_map/gather | solution.py:128
  78.2 2.7 %gather_fusion.2 = bf16[4,256,256]{2,1,0:T(8,128)(2,1)} fusion(bf16[8,256,256]{2,1,0:T(8,128)(2,1)} %bitcast.305, s32[1024]{0:T(1024)} %pad_clamp_fusion.11), kind=kCustom, calls=%fused_computation.2 | custom fusion | bytes 1048592 | tf_op jit(solution)/shard_map/gather | solution.py:128
  80.9 2.7 %gather_fusion.1 = bf16[4,256,256]{2,1,0:T(8,128)(2,1)} fusion(bf16[8,256,256]{2,1,0:T(8,128)(2,1)} %bitcast.306, s32[1024]{0:T(1024)} %pad_clamp_fusion.12), kind=kCustom, calls=%fused_computation.1 | custom fusion | bytes 1048592 | tf_op jit(solution)/shard_map/gather | solution.py:128
  83.6 2.8 %gather_fusion = bf16[4,256,256]{2,1,0:T(8,128)(2,1)} fusion(bf16[8,256,256]{2,1,0:T(8,128)(2,1)} %bitcast.307, s32[1024]{0:T(1024)} %pad_clamp_fusion.13), kind=kCustom, calls=%fused_computation | custom fusion | bytes 1048592 | tf_op jit(solution)/shard_map/gather | solution.py:128
  86.4 1.5 gather_fusion.8
  87.9 1.5 gather_fusion.7
  89.4 1.5 gather_fusion.6
  91.7 1.6 collective-permute-start.21
  93.3 1.5 bitcast_dynamic-update-slice_fusion.6
  94.8 2.5 %collective-permute-done.21 = bf16[4,16,448]{2,1,0:T(8,128)(2,1)S(1)} collective-permute-done((bf16[4,16,448]{2,1,0:T(8,128)(2,1)S(1)}, bf16[4,16,448]{2,1,0:T(8,128)(2,1)S(1)}, u32[]{:S(2)}, u32[]{:S(2)}) %collective-permute-start.21) | collective-permute-done | bytes 57376 | tf_op jit(solution)/shard_map/ppermute | solution.py:148
  98.1 1.5 bitcast_dynamic-update-slice_fusion.4
  99.6 2.0 collective-permute-start.4
  101.6 1.5 bitcast_dynamic-update-slice_fusion.3
  103.1 1.2 collective-permute-start.5
  104.3 1.5 bitcast_dynamic-update-slice_fusion.2
  105.9 5.0 %collective-permute-start.11 = (bf16[4,256,256]{2,1,0:T(8,128)(2,1)}, bf16[4,256,256]{2,1,0:T(8,128)(2,1)}, u32[]{:S(2)}, u32[]{:S(2)}) collective-permute-start(bf16[4,256,256]{2,1,0:T(8,128)(2,1)} %gather_fusion.7), channel_id=1, source_target_pairs={{0,64},{32,96},{64,0},{96,32},{1,65},{33,97},{65,1},{97,33},{2,66}... | collective-permute-start | bytes 1572872 | tf_op jit(solution)/shard_map/ppermute | solution.py:134
  110.9 14.1 %collective-permute-done.3 = bf16[4,256,256]{2,1,0:T(8,128)(2,1)S(1)} collective-permute-done((bf16[4,256,256]{2,1,0:T(8,128)(2,1)}, bf16[4,256,256]{2,1,0:T(8,128)(2,1)S(1)}, u32[]{:S(2)}, u32[]{:S(2)}) %collective-permute-start.3) | collective-permute-done | bytes 524320 | tf_op jit(solution)/shard_map/ppermute | solution.py:134
  124.9 1.8 collective-permute-start.12
  126.7 1.5 bitcast_dynamic-update-slice_fusion.1
  128.8 1.7 gather_fusion.16
  130.9 1.3 dot_general.31
  132.2 3.1 %pad_maximum_fusion = bf16[4,4,256,256]{3,2,1,0:T(8,128)(2,1)} fusion(bf16[1,4,256,256]{3,2,1,0:T(8,128)(2,1)} %bitcast.20, bf16[1,4,256,256]{3,2,1,0:T(8,128)(2,1)} %bitcast.16, bf16[1,4,256,256]{3,2,1,0:T(8,128)(2,1)} %bitcast.319, bf16[1,4,256,256]{3,2,1,0:T(8,128)(2,1)} %bitcast.316), kind=kLoop, calls=%fused_computation.32 | loop fusion | flops 3145728 | bytes 4194304 | tf_op jit(solution)/shard_map/stack | solution.py:136
  135.3 2.2 gather_fusion.4
  138.7 3.0 %pad_maximum_fusion.1 = bf16[4,4,256,256]{3,2,1,0:T(8,128)(2,1)} fusion(bf16[1,4,256,256]{3,2,1,0:T(8,128)(2,1)} %bitcast.54, bf16[1,4,256,256]{3,2,1,0:T(8,128)(2,1)} %bitcast.50, bf16[1,4,256,256]{3,2,1,0:T(8,128)(2,1)} %bitcast.46, bf16[1,4,256,256]{3,2,1,0:T(8,128)(2,1)S(1)} %bitcast.315), kind=kLoop, calls=%fused_computation.33 | loop fusion | flops 3145728 | bytes 4194304 | tf_op jit(solution)/shard_map/stack | solution.py:136
  141.7 3.0 %gather_fusion.9 = bf16[4,256,256]{2,1,0:T(8,128)(2,1)} fusion(bf16[4,4,256,256]{3,2,1,0:T(8,128)(2,1)} %pad_maximum_fusion.1, s32[4]{0:T(128)S(1)} %copy-done.17), kind=kCustom, calls=%fused_computation.9 | custom fusion | bytes 1048608 | tf_op jit(solution)/shard_map/gather | solution.py:139
  144.7 3.0 %fusion.2 = f32[512]{0:T(512)S(1)} fusion(bf16[512,3584]{0,1:T(8,128)(2,1)} %all-gather.2.cloned.1.call-done), kind=kLoop, calls=%fused_computation.23 | loop fusion | flops 5504512 | bytes 3672064 | tf_op jit(solution)/shard_map/reduce_sum | solution.py:191
  147.8 1.6 fusion.4
  149.4 1.8 copy-done.2
  151.2 1.9 convolution_convert_fusion.1
  153.0 1.8 copy.54
  154.8 2.1 collective-permute-start.6
  157.0 3.8 %convolution_bitcast_fusion = f32[512,1,256]{0,2,1:T(8,128)S(1)} fusion(bf16[512,3584]{0,1:T(8,128)(2,1)} %copy-done.2, bf16[3584,256]{1,0:T(8,128)(2,1)} %param.19), kind=kOutput, calls=%fused_computation.38 | convolution fusion | flops 939524096 | bytes 6029312 | tf_op jit(solution)/shard_map/dot_general | solution.py:215
  160.7 1.2 fusion.35
  162.6 1.8 copy.57
  164.5 3.9 %collective-permute-start.13 = (bf16[512,256]{0,1:T(8,128)(2,1)}, bf16[512,256]{0,1:T(8,128)(2,1)}, u32[]{:S(2)}, u32[]{:S(2)}) collective-permute-start(bf16[512,256]{0,1:T(8,128)(2,1)} %maximum_bitcast_fusion.6), channel_id=1, source_target_pairs={{0,8},{8,16},{16,24},{24,32},{32,40},{40,48},{48,56},{56,64},{64,7... | collective-permute-start | bytes 786440 | tf_op jit(solution)/shard_map/ppermute | solution.py:16
  168.3 6.2 %fusion.162 = f32[512,512]{0,1:T(8,128)} fusion(bf16[512,3584]{0,1:T(8,128)(2,1)} %copy-done.2, bf16[3584,512]{1,0:T(8,128)(2,1)} %param.18), kind=kOutput, calls=%fused_computation.363 | convolution fusion | flops 1879048192 | bytes 8388608 | tf_op jit(solution)/shard_map/dot_general | solution.py:210
  174.6 3.3 %fusion.13 = f32[512,512]{0,1:T(8,128)S(1)} fusion(f32[512,512]{0,1:T(8,128)} %fusion.162, bf16[64,512]{1,0:T(8,128)(2,1)S(1)} %bitcast.320, bf16[512,64]{0,1:T(8,128)(2,1)S(1)} %bitcast.321, bf16[64,3584]{1,0:T(8,128)(2,1)S(1)} %copy-done.6, bf16[512,3584]{0,1:T(8,128)(2,1)} %copy-done.2), kind=kOutput, calls=%fused_computation.37 | convolution fusion | flops 269025280 | bytes 6356992 | tf_op jit(solution)/shard_map/dot_general | solution.py:204
  179.0 1.3 copy.69
  180.4 2.1 copy.68
  182.4 2.1 subtract_convert_fusion
  185.7 3.1 %fusion.5 = (f32[2,512]{1,0:T(2,128)S(1)}, f32[2048,512,2]{1,0,2:T(8,128)S(1)}) fusion(pred[512,2048]{0,1:T(8,128)(4,1)S(1)} %copy-done.5, bf16[512,2,128]{2,0,1:T(8,128)(2,1)} %get-tuple-element.20, bf16[512,2,128]{2,0,1:T(8,128)(2,1)} %get-tuple-element.19, bf16[512,256]{1,0:T(8,128)(2,1)} %copy.57, bf16[512,256]{1,0:T(8,128)(2,1)S(1)} %copy.56, ...), kind=kOutput, calls=%fused_computation.26 | convolution fusion | flops 1084226560 | bytes 11014144 | tf_op jit(solution)/shard_map/tkrd,skd->krts/dot_general | solution.py:84
  188.7 2.0 fusion
  190.7 1.3 copy-done.4
  192.0 1.8 copy.53
  193.8 6.3 %divide_convert_fusion = bf16[512,1,2,256]{0,3,2,1:T(8,128)(2,1)S(1)} fusion(f32[2048,512,2]{1,0,2:T(8,128)} %copy-done.4, f32[2,512]{1,0:T(2,128)S(1)} %get-tuple-element.54, pred[512,2048]{0,1:T(8,128)(4,1)S(1)} %copy-done.5, bf16[512,256]{0,1:T(8,128)(2,1)} %copy.54, bf16[512,256]{0,1:T(8,128)(2,1)} %copy.53, bf16[1024,256]{0,1:T(8,128)(2,1)S(1)} %copy-done.7, ...), kind=kOutput, calls=%fused_computation.55 | convolution fusion | flops 1085800448 | bytes 11018240 | tf_op jit(solution)/shard_map/krts,skd->tkrd/dot_general | solution.py:91
  200.1 3.9 %convolution_convert_fusion = bf16[512,3584]{0,1:T(8,128)(2,1)} fusion(bf16[512,512]{0,1:T(8,128)(2,1)S(1)} %bitcast.334, bf16[512,3584]{1,0:T(8,128)(2,1)S(1)} %copy-done.22), kind=kOutput, calls=%fused_computation.27 | convolution fusion | flops 1880883200 | bytes 7864320 | tf_op jit(solution)/shard_map/dot_general | solution.py:237
  204.1 36.7 %reduce-scatter.2.cloned.1.call-done = bf16[512,448]{0,1:T(8,128)(2,1)} async-done(((bf16[512,3584]{0,1:T(8,128)(2,1)}), bf16[512,448]{0,1:T(8,128)(2,1)}) %reduce-scatter.2.cloned.1.call-update) | async-done | bytes 458768 | tf_op jit(solution)/shard_map/reduce_scatter | solution.py:238
  (152 shorter events, 34.4 us)
Async XLA Ops:
  6.5 144.6 %copy-start = (bf16[3584,256]{1,0:T(8,128)(2,1)S(1)}, bf16[3584,256]{1,0:T(8,128)(2,1)}, u32[]{:S(2)}) copy-start(bf16[3584,256]{1,0:T(8,128)(2,1)} %param.20) | copy-start | bytes 5505028
  6.5 13.5 %copy-start.1 = (s32[64]{0:T(128)S(1)}, s32[64]{0:T(128)}, u32[]{:S(2)}) copy-start(s32[64]{0:T(128)} %param.25) | copy-start | bytes 772
  6.5 138.1 %all-gather.2.cloned.1.call-start = ((), (), s32[]{:S(2)}) async-start(), calls=%async_computation.1 | async-start | bytes 4128768 | tf_op jit(solution)/shard_map/all_gather | solution.py:188
  7.7 35.1 %collective-permute-start.15 = (bf16[4,16,960]{2,1,0:T(8,128)(2,1)S(1)}, bf16[4,16,960]{2,1,0:T(8,128)(2,1)S(1)}, u32[]{:S(2)}, u32[]{:S(2)}) collective-permute-start(bf16[4,16,960]{2,1,0:T(8,128)(2,1)S(1)} %get-tuple-element.26), channel_id=1, source_target_pairs={{0,16},{8,24},{16,0},{24,8},{1,17},{9,25},{17,1},{25,9},{2,18},{10... | collective-permute-start | bytes 368648 | tf_op jit(solution)/shard_map/ppermute | solution.py:107
  11.7 31.0 %collective-permute-start.14 = (bf16[4,16,960]{2,1,0:T(8,128)(2,1)S(1)}, bf16[4,16,960]{2,1,0:T(8,128)(2,1)S(1)}, u32[]{:S(2)}, u32[]{:S(2)}) collective-permute-start(bf16[4,16,960]{2,1,0:T(8,128)(2,1)S(1)} %get-tuple-element.26), channel_id=1, source_target_pairs={{0,8},{8,16},{16,24},{24,0},{1,9},{9,17},{17,25},{25,1},{2,10},{10... | collective-permute-start | bytes 368648 | tf_op jit(solution)/shard_map/ppermute | solution.py:107
  12.7 30.0 %collective-permute-start.16 = (bf16[4,16,960]{2,1,0:T(8,128)(2,1)S(1)}, bf16[4,16,960]{2,1,0:T(8,128)(2,1)S(1)}, u32[]{:S(2)}, u32[]{:S(2)}) collective-permute-start(bf16[4,16,960]{2,1,0:T(8,128)(2,1)S(1)} %get-tuple-element.26), channel_id=1, source_target_pairs={{0,24},{8,0},{16,8},{24,16},{1,25},{9,1},{17,9},{25,17},{2,26},{10... | collective-permute-start | bytes 368648 | tf_op jit(solution)/shard_map/ppermute | solution.py:107
  14.9 46.5 %collective-permute-start.7 = (bf16[2,256,256]{2,1,0:T(8,128)(2,1)}, bf16[2,256,256]{2,1,0:T(8,128)(2,1)S(1)}, u32[]{:S(2)}, u32[]{:S(2)}) collective-permute-start(bf16[2,256,256]{2,1,0:T(8,128)(2,1)} %param.30), channel_id=1, source_target_pairs={{0,8},{8,16},{16,24},{24,0},{1,9},{9,17},{17,25},{25,1},{2,10},{10... | collective-permute-start | bytes 786440 | tf_op jit(solution)/shard_map/ppermute | solution.py:107
  14.9 47.7 %collective-permute-start.9 = (bf16[2,256,256]{2,1,0:T(8,128)(2,1)}, bf16[2,256,256]{2,1,0:T(8,128)(2,1)}, u32[]{:S(2)}, u32[]{:S(2)}) collective-permute-start(bf16[2,256,256]{2,1,0:T(8,128)(2,1)} %param.30), channel_id=1, source_target_pairs={{0,24},{8,0},{16,8},{24,16},{1,25},{9,1},{17,9},{25,17},{2,26},{10... | collective-permute-start | bytes 786440 | tf_op jit(solution)/shard_map/ppermute | solution.py:107
  18.2 222.5 %reduce-scatter.2.cloned.1.call-start = ((), (), s32[]{:S(2)}) async-start(), calls=%async_computation.2 | async-start | bytes 4128768 | tf_op jit(solution)/shard_map/reduce_scatter | solution.py:238
  18.4 19.1 %copy-start.20 = (f32[128]{0:T(128)}, f32[128]{0:T(128)S(1)}, u32[]{:S(2)}) copy-start(f32[128]{0:T(128)S(1)} %multiply_power_fusion) | copy-start | bytes 1540
  20.0 2.2 copy-start.19
  20.0 2.7 %copy-start.18 = (s32[16,4]{0,1:T(4,128)S(1)}, s32[16,4]{0,1:T(4,128)}, u32[]{:S(2)}) copy-start(s32[16,4]{0,1:T(4,128)} %param.29) | copy-start | bytes 772
  20.1 8.9 %copy-start.23 = (s32[16]{0:T(128)S(1)}, s32[16]{0:T(128)}, u32[]{:S(2)}) copy-start(s32[16]{0:T(128)} %param.27) | copy-start | bytes 196
  20.9 34.4 %copy-start.9 = (bf16[2,256,256]{2,1,0:T(8,128)(2,1)S(1)}, bf16[2,256,256]{2,1,0:T(8,128)(2,1)}, u32[]{:S(2)}) copy-start(bf16[2,256,256]{2,1,0:T(8,128)(2,1)} %param.30) | copy-start | bytes 786436
  20.9 35.5 %copy-start.10 = (bf16[2,256,256]{2,1,0:T(8,128)(2,1)S(1)}, bf16[2,256,256]{2,1,0:T(8,128)(2,1)}, u32[]{:S(2)}) copy-start(bf16[2,256,256]{2,1,0:T(8,128)(2,1)} %param.31) | copy-start | bytes 786436
  21.6 21.2 %copy-start.16 = (pred[16,4]{1,0:T(8,128)(4,1)}, pred[16,4]{1,0:T(8,128)(4,1)S(1)}, u32[]{:S(2)}) copy-start(pred[16,4]{1,0:T(8,128)(4,1)S(1)} %get-tuple-element.15) | copy-start | bytes 196
  42.7 0.7 copy-start.12
  42.7 0.7 copy-start.13
  47.2 8.1 %collective-permute-start.17 = (bf16[4,16,960]{2,1,0:T(8,128)(2,1)}, bf16[4,16,960]{2,1,0:T(8,128)(2,1)}, u32[]{:S(2)}, u32[]{:S(2)}) collective-permute-start(bf16[4,16,960]{2,1,0:T(8,128)(2,1)} %gather_fusion.12), channel_id=1, source_target_pairs={{0,32},{32,64},{64,96},{96,0},{1,33},{33,65},{65,97},{97,1},{2,34}... | collective-permute-start | bytes 368648 | tf_op jit(solution)/shard_map/ppermute | solution.py:134
  48.7 7.7 %collective-permute-start.18 = (bf16[4,16,960]{2,1,0:T(8,128)(2,1)S(1)}, bf16[4,16,960]{2,1,0:T(8,128)(2,1)}, u32[]{:S(2)}, u32[]{:S(2)}) collective-permute-start(bf16[4,16,960]{2,1,0:T(8,128)(2,1)S(1)} %gather_fusion.13), channel_id=1, source_target_pairs={{0,64},{32,96},{64,0},{96,32},{1,65},{33,97},{65,1},{97,33},{2,66}... | collective-permute-start | bytes 368648 | tf_op jit(solution)/shard_map/ppermute | solution.py:134
  51.4 5.5 %collective-permute-start.19 = (bf16[4,16,960]{2,1,0:T(8,128)(2,1)S(1)}, bf16[4,16,960]{2,1,0:T(8,128)(2,1)}, u32[]{:S(2)}, u32[]{:S(2)}) collective-permute-start(bf16[4,16,960]{2,1,0:T(8,128)(2,1)S(1)} %gather_fusion.14), channel_id=1, source_target_pairs={{0,96},{32,0},{64,32},{96,64},{1,97},{33,1},{65,33},{97,65},{2,98}... | collective-permute-start | bytes 368648 | tf_op jit(solution)/shard_map/ppermute | solution.py:134
  55.3 10.4 %collective-permute-start.8 = (bf16[2,256,256]{2,1,0:T(8,128)(2,1)S(1)}, bf16[2,256,256]{2,1,0:T(8,128)(2,1)}, u32[]{:S(2)}, u32[]{:S(2)}) collective-permute-start(bf16[2,256,256]{2,1,0:T(8,128)(2,1)S(1)} %copy-done.9), channel_id=1, source_target_pairs={{0,16},{8,24},{16,0},{24,8},{1,17},{9,25},{17,1},{25,9},{2,18},{10... | collective-permute-start | bytes 786440 | tf_op jit(solution)/shard_map/ppermute | solution.py:107
  56.3 13.3 %collective-permute-start = (bf16[2,256,256]{2,1,0:T(8,128)(2,1)S(1)}, bf16[2,256,256]{2,1,0:T(8,128)(2,1)}, u32[]{:S(2)}, u32[]{:S(2)}) collective-permute-start(bf16[2,256,256]{2,1,0:T(8,128)(2,1)S(1)} %copy-done.10), channel_id=1, source_target_pairs={{0,32},{32,64},{64,96},{96,0},{1,33},{33,65},{65,97},{97,1},{2,34}... | collective-permute-start | bytes 786440 | tf_op jit(solution)/shard_map/ppermute | solution.py:107
  56.9 16.0 %collective-permute-start.2 = (bf16[2,256,256]{2,1,0:T(8,128)(2,1)S(1)}, bf16[2,256,256]{2,1,0:T(8,128)(2,1)}, u32[]{:S(2)}, u32[]{:S(2)}) collective-permute-start(bf16[2,256,256]{2,1,0:T(8,128)(2,1)S(1)} %copy-done.10), channel_id=1, source_target_pairs={{0,96},{32,0},{64,32},{96,64},{1,97},{33,1},{65,33},{97,65},{2,98}... | collective-permute-start | bytes 786440 | tf_op jit(solution)/shard_map/ppermute | solution.py:107
  61.5 4.2 %copy-start.11 = (bf16[2,256,256]{2,1,0:T(8,128)(2,1)}, bf16[2,256,256]{2,1,0:T(8,128)(2,1)S(1)}, u32[]{:S(2)}) copy-start(bf16[2,256,256]{2,1,0:T(8,128)(2,1)S(1)} %collective-permute-done.7) | copy-start | bytes 786436
  61.5 11.4 %collective-permute-start.1 = (bf16[2,256,256]{2,1,0:T(8,128)(2,1)S(1)}, bf16[2,256,256]{2,1,0:T(8,128)(2,1)S(1)}, u32[]{:S(2)}, u32[]{:S(2)}) collective-permute-start(bf16[2,256,256]{2,1,0:T(8,128)(2,1)S(1)} %copy-done.10), channel_id=1, source_target_pairs={{0,64},{32,96},{64,0},{96,32},{1,65},{33,97},{65,1},{97,33},{2,66}... | collective-permute-start | bytes 786440 | tf_op jit(solution)/shard_map/ppermute | solution.py:107
  62.6 43.1 %collective-permute-start.25 = (bf16[4,16,448]{2,1,0:T(8,128)(2,1)S(1)}, bf16[4,16,448]{2,1,0:T(8,128)(2,1)}, u32[]{:S(2)}, u32[]{:S(2)}) collective-permute-start(bf16[4,16,448]{2,1,0:T(8,128)(2,1)S(1)} %slice.70), channel_id=1, source_target_pairs={{0,6},{1,7},{2,0},{3,1},{4,2},{5,3},{6,4},{7,5},{8,14},{9,15},{10,... | collective-permute-start | bytes 172040 | tf_op jit(solution)/shard_map/ppermute | solution.py:148
  65.7 37.4 %collective-permute-start.24 = (bf16[4,16,448]{2,1,0:T(8,128)(2,1)S(1)}, bf16[4,16,448]{2,1,0:T(8,128)(2,1)}, u32[]{:S(2)}, u32[]{:S(2)}) collective-permute-start(bf16[4,16,448]{2,1,0:T(8,128)(2,1)S(1)} %slice.70), channel_id=1, source_target_pairs={{0,5},{1,6},{2,7},{3,0},{4,1},{5,2},{6,3},{7,4},{8,13},{9,14},{10,... | collective-permute-start | bytes 172040 | tf_op jit(solution)/shard_map/ppermute | solution.py:148
  69.6 29.9 %collective-permute-start.23 = (bf16[4,16,448]{2,1,0:T(8,128)(2,1)S(1)}, bf16[4,16,448]{2,1,0:T(8,128)(2,1)}, u32[]{:S(2)}, u32[]{:S(2)}) collective-permute-start(bf16[4,16,448]{2,1,0:T(8,128)(2,1)S(1)} %slice.70), channel_id=1, source_target_pairs={{0,4},{1,5},{2,6},{3,7},{4,0},{5,1},{6,2},{7,3},{8,12},{9,13},{10,... | collective-permute-start | bytes 172040 | tf_op jit(solution)/shard_map/ppermute | solution.py:148
  72.8 25.3 %collective-permute-start.22 = (bf16[4,16,448]{2,1,0:T(8,128)(2,1)S(1)}, bf16[4,16,448]{2,1,0:T(8,128)(2,1)}, u32[]{:S(2)}, u32[]{:S(2)}) collective-permute-start(bf16[4,16,448]{2,1,0:T(8,128)(2,1)S(1)} %slice.70), channel_id=1, source_target_pairs={{0,3},{1,4},{2,5},{3,6},{4,7},{5,0},{6,1},{7,2},{8,11},{9,12},{10,... | collective-permute-start | bytes 172040 | tf_op jit(solution)/shard_map/ppermute | solution.py:148
  72.8 18.8 %collective-permute-start.20 = (bf16[4,16,448]{2,1,0:T(8,128)(2,1)S(1)}, bf16[4,16,448]{2,1,0:T(8,128)(2,1)}, u32[]{:S(2)}, u32[]{:S(2)}) collective-permute-start(bf16[4,16,448]{2,1,0:T(8,128)(2,1)S(1)} %slice.70), channel_id=1, source_target_pairs={{0,1},{1,2},{2,3},{3,4},{4,5},{5,6},{6,7},{7,0},{8,9},{9,10},{10,1... | collective-permute-start | bytes 172040 | tf_op jit(solution)/shard_map/ppermute | solution.py:148
  91.7 5.6 %collective-permute-start.21 = (bf16[4,16,448]{2,1,0:T(8,128)(2,1)S(1)}, bf16[4,16,448]{2,1,0:T(8,128)(2,1)S(1)}, u32[]{:S(2)}, u32[]{:S(2)}) collective-permute-start(bf16[4,16,448]{2,1,0:T(8,128)(2,1)S(1)} %slice.70), channel_id=1, source_target_pairs={{0,2},{1,3},{2,4},{3,5},{4,6},{5,7},{6,0},{7,1},{8,10},{9,11},{10,... | collective-permute-start | bytes 172040 | tf_op jit(solution)/shard_map/ppermute | solution.py:148
  97.3 8.6 %collective-permute-start.26 = (bf16[4,16,448]{2,1,0:T(8,128)(2,1)S(1)}, bf16[4,16,448]{2,1,0:T(8,128)(2,1)S(1)}, u32[]{:S(2)}, u32[]{:S(2)}) collective-permute-start(bf16[4,16,448]{2,1,0:T(8,128)(2,1)S(1)} %slice.70), channel_id=1, source_target_pairs={{0,7},{1,0},{2,1},{3,2},{4,3},{5,4},{6,5},{7,6},{8,15},{9,8},{10,9... | collective-permute-start | bytes 172040 | tf_op jit(solution)/shard_map/ppermute | solution.py:148
  98.1 26.8 %collective-permute-start.3 = (bf16[4,256,256]{2,1,0:T(8,128)(2,1)}, bf16[4,256,256]{2,1,0:T(8,128)(2,1)S(1)}, u32[]{:S(2)}, u32[]{:S(2)}) collective-permute-start(bf16[4,256,256]{2,1,0:T(8,128)(2,1)} %gather_fusion.1), channel_id=1, source_target_pairs={{0,8},{8,16},{16,24},{24,0},{1,9},{9,17},{17,25},{25,1},{2,10},{10... | collective-permute-start | bytes 1572872 | tf_op jit(solution)/shard_map/ppermute | solution.py:134
  99.6 32.6 %collective-permute-start.4 = (bf16[4,256,256]{2,1,0:T(8,128)(2,1)}, bf16[4,256,256]{2,1,0:T(8,128)(2,1)}, u32[]{:S(2)}, u32[]{:S(2)}) collective-permute-start(bf16[4,256,256]{2,1,0:T(8,128)(2,1)} %gather_fusion.2), channel_id=1, source_target_pairs={{0,16},{8,24},{16,0},{24,8},{1,17},{9,25},{17,1},{25,9},{2,18},{10... | collective-permute-start | bytes 1572872 | tf_op jit(solution)/shard_map/ppermute | solution.py:134
  103.1 29.1 %collective-permute-start.5 = (bf16[4,256,256]{2,1,0:T(8,128)(2,1)}, bf16[4,256,256]{2,1,0:T(8,128)(2,1)}, u32[]{:S(2)}, u32[]{:S(2)}) collective-permute-start(bf16[4,256,256]{2,1,0:T(8,128)(2,1)} %gather_fusion.3), channel_id=1, source_target_pairs={{0,24},{8,0},{16,8},{24,16},{1,25},{9,1},{17,9},{25,17},{2,26},{10... | collective-permute-start | bytes 1572872 | tf_op jit(solution)/shard_map/ppermute | solution.py:134
  105.8 32.8 %collective-permute-start.10 = (bf16[4,256,256]{2,1,0:T(8,128)(2,1)}, bf16[4,256,256]{2,1,0:T(8,128)(2,1)}, u32[]{:S(2)}, u32[]{:S(2)}) collective-permute-start(bf16[4,256,256]{2,1,0:T(8,128)(2,1)} %gather_fusion.6), channel_id=1, source_target_pairs={{0,32},{32,64},{64,96},{96,0},{1,33},{33,65},{65,97},{97,1},{2,34}... | collective-permute-start | bytes 1572872 | tf_op jit(solution)/shard_map/ppermute | solution.py:134
  105.9 32.7 %collective-permute-start.11 = (bf16[4,256,256]{2,1,0:T(8,128)(2,1)}, bf16[4,256,256]{2,1,0:T(8,128)(2,1)}, u32[]{:S(2)}, u32[]{:S(2)}) collective-permute-start(bf16[4,256,256]{2,1,0:T(8,128)(2,1)} %gather_fusion.7), channel_id=1, source_target_pairs={{0,64},{32,96},{64,0},{96,32},{1,65},{33,97},{65,1},{97,33},{2,66}... | collective-permute-start | bytes 1572872 | tf_op jit(solution)/shard_map/ppermute | solution.py:134
  124.9 3.3 %copy-start.8 = (bf16[4,256,256]{2,1,0:T(8,128)(2,1)}, bf16[4,256,256]{2,1,0:T(8,128)(2,1)S(1)}, u32[]{:S(2)}) copy-start(bf16[4,256,256]{2,1,0:T(8,128)(2,1)S(1)} %collective-permute-done.3) | copy-start | bytes 1572868
  124.9 13.8 %collective-permute-start.12 = (bf16[4,256,256]{2,1,0:T(8,128)(2,1)}, bf16[4,256,256]{2,1,0:T(8,128)(2,1)}, u32[]{:S(2)}, u32[]{:S(2)}) collective-permute-start(bf16[4,256,256]{2,1,0:T(8,128)(2,1)} %gather_fusion.8), channel_id=1, source_target_pairs={{0,96},{32,0},{64,32},{96,64},{1,97},{33,1},{65,33},{97,65},{2,98}... | collective-permute-start | bytes 1572872 | tf_op jit(solution)/shard_map/ppermute | solution.py:134
  128.8 6.5 %copy-start.15 = (s32[4]{0:T(128)S(1)}, s32[4]{0:T(128)}, u32[]{:S(2)}) copy-start(s32[4]{0:T(128)} %get-tuple-element.8) | copy-start | bytes 52
  135.3 6.4 %copy-start.17 = (s32[4]{0:T(128)S(1)}, s32[4]{0:T(128)}, u32[]{:S(2)}) copy-start(s32[4]{0:T(128)} %fusion.152) | copy-start | bytes 52
  138.7 9.0 %copy-start.14 = (f32[3584]{0:T(1024)S(1)}, f32[3584]{0:T(1024)}, u32[]{:S(2)}) copy-start(f32[3584]{0:T(1024)} %param.17) | copy-start | bytes 43012
  144.6 3.1 %copy-start.3 = (bf16[512,3584]{0,1:T(8,128)(2,1)S(1)}, bf16[512,3584]{0,1:T(8,128)(2,1)}, u32[]{:S(2)}) copy-start(bf16[512,3584]{0,1:T(8,128)(2,1)} %all-gather.2.cloned.1.call-done) | copy-start | bytes 11010052
  149.4 1.8 copy-start.2
  154.8 5.9 %copy-start.21 = (f32[128]{0:T(128)S(1)}, f32[128]{0:T(128)}, u32[]{:S(2)}) copy-start(f32[128]{0:T(128)} %copy-done.20) | copy-start | bytes 1540
  154.8 37.2 %collective-permute-start.6 = (bf16[512,256]{1,0:T(8,128)(2,1)}, bf16[512,256]{1,0:T(8,128)(2,1)}, u32[]{:S(2)}, u32[]{:S(2)}) collective-permute-start(bf16[512,256]{1,0:T(8,128)(2,1)} %convolution_convert_fusion.1), channel_id=1, source_target_pairs={{0,8},{8,16},{16,24},{24,32},{32,40},{40,48},{48,56},{56,64},{64,7... | collective-permute-start | bytes 786440 | tf_op jit(solution)/shard_map/ppermute | solution.py:16
  164.5 10.1 %copy-start.6 = (bf16[64,3584]{1,0:T(8,128)(2,1)S(1)}, bf16[64,3584]{1,0:T(8,128)(2,1)}, u32[]{:S(2)}) copy-start(bf16[64,3584]{1,0:T(8,128)(2,1)} %dot_general.31) | copy-start | bytes 1376260
  164.5 20.1 %collective-permute-start.13 = (bf16[512,256]{0,1:T(8,128)(2,1)}, bf16[512,256]{0,1:T(8,128)(2,1)}, u32[]{:S(2)}, u32[]{:S(2)}) collective-permute-start(bf16[512,256]{0,1:T(8,128)(2,1)} %maximum_bitcast_fusion.6), channel_id=1, source_target_pairs={{0,8},{8,16},{16,24},{24,32},{32,40},{40,48},{48,56},{56,64},{64,7... | collective-permute-start | bytes 786440 | tf_op jit(solution)/shard_map/ppermute | solution.py:16
  179.0 6.6 %copy-start.5 = (pred[512,2048]{0,1:T(8,128)(4,1)S(1)}, pred[512,2048]{0,1:T(8,128)(4,1)}, u32[]{:S(2)}) copy-start(pred[512,2048]{0,1:T(8,128)(4,1)} %pad_add_fusion) | copy-start | bytes 3145732
  188.7 3.3 %copy-start.4 = (f32[2048,512,2]{1,0,2:T(8,128)}, f32[2048,512,2]{1,0,2:T(8,128)S(1)}, u32[]{:S(2)}) copy-start(f32[2048,512,2]{1,0,2:T(8,128)S(1)} %get-tuple-element.55) | copy-start | bytes 25165828
  188.7 5.1 %copy-start.7 = (bf16[1024,256]{0,1:T(8,128)(2,1)S(1)}, bf16[1024,256]{0,1:T(8,128)(2,1)}, u32[]{:S(2)}) copy-start(bf16[1024,256]{0,1:T(8,128)(2,1)} %copy.66) | copy-start | bytes 1572868
  193.8 6.3 %copy-start.22 = (bf16[512,3584]{1,0:T(8,128)(2,1)S(1)}, bf16[512,3584]{1,0:T(8,128)(2,1)}, u32[]{:S(2)}) copy-start(bf16[512,3584]{1,0:T(8,128)(2,1)} %param.21) | copy-start | bytes 11010052
Sparse Core Ops, SparseCore 0:
  18.3 28.8 all-gather.1
  204.2 36.4 reduce-scatter.1

commit v2 on v1

--- a/solution.py
+++ b/solution.py
@@ -101,58 +101,48 @@
 SIDE = 4
 
 
-def ring_gather(value, axis):
-    held = [value]
-    for step in range(1, SIDE):
-        held.append(lax.ppermute(value, axis, [(i, (i + step) % SIDE) for i in range(SIDE)]))
-    return jnp.stack(held)
-
-
 def group_of(first, a_coord, b_coord):
     return b_coord * SIDE + a_coord if first == "gz" else a_coord * SIDE + b_coord
 
 
-def route(local, wanted, first, second):
-    per_owner = local.shape[0]
+def route(locals_, wanteds, first, second):
     coords = {"gx": lax.axis_index("gx"), "gz": lax.axis_index("gz")}
     own_a, own_b = coords[first], coords[second]
-    owner = wanted // per_owner
-    owner_coords = {"gx": owner // SIDE, "gz": owner % SIDE}
-    owner_a, owner_b = owner_coords[first], owner_coords[second]
-    part = wanted % per_owner
-    held = ring_gather(local, first).reshape(SIDE * per_owner, *local.shape[1:])
-
-    def pick(requester_b):
-        asker = group_of(first, own_a, requester_b)
-        shift = (own_a - owner_a[asker]) % SIDE
-        return held[shift * per_owner + part[asker]]
-
-    received = [pick(own_b)]
-    for step in range(1, SIDE):
-        payload = pick((own_b + step) % SIDE)
-        received.append(
-            lax.ppermute(payload, second, [(i, (i + step) % SIDE) for i in range(SIDE)])
+    items = [local.reshape(local.shape[0], -1) for local in locals_]
+    packed = jnp.concatenate([item.reshape(-1) for item in items])
+    held_all = lax.all_gather(packed, first, axis=0, tiled=False)
+    dests = group_of(first, own_a, jnp.arange(SIDE))
+    me = group_of(first, own_a, own_b)
+    payloads, picks, offset = [], [], 0
+    for item, wanted in zip(items, wanteds):
+        per_owner, width = item.shape
+        held = held_all[:, offset:offset + per_owner * width].reshape(SIDE * per_owner, width)
+        offset += per_owner * width
+        owner = wanted // per_owner
+        owner_a = (owner // SIDE, owner % SIDE)[first == "gz"]
+        owner_b = (owner // SIDE, owner % SIDE)[second == "gz"]
+        source = owner_a[dests] * per_owner + (wanted % per_owner)[dests]
+        select = (source[..., None] == jnp.arange(SIDE * per_owner)).astype(item.dtype)
+        payloads.append(
+            jnp.einsum("dsj,jn->dsn", select, held, preferred_element_type=jnp.float32).astype(
+                item.dtype
+            )
         )
-    stacked = jnp.stack(received)
-    me = group_of(first, own_a, own_b)
-    came_from = (own_b - owner_b[me]) % SIDE
-    return stacked[came_from, jnp.arange(wanted.shape[1])]
-
-
-def gather_model(value, axis):
-    count = 8
-    model_at = lax.axis_index(("my", "mc"))
-    held = [value]
-    for step in range(1, count):
-        held.append(
-            lax.ppermute(value, ("my", "mc"), [(i, (i + step) % count) for i in range(count)])
-        )
-    held = jnp.stack(held)
-    ordered = held[(model_at - jnp.arange(count)) % count]
-    moved = jnp.moveaxis(ordered, 0, axis)
-    shape = list(value.shape)
-    shape[axis] = shape[axis] * count
-    return moved.reshape(shape)
+        slots = wanted.shape[1]
+        picks.append(owner_b[me] * slots + jnp.arange(slots))
+    widths = [p.shape[2] for p in payloads]
+    received = lax.all_to_all(
+        jnp.concatenate(payloads, axis=2), second, split_axis=0, concat_axis=0, tiled=True
+    )
+    received = received.reshape(SIDE * received.shape[1], -1)
+    results, offset = [], 0
+    for local, width, pick in zip(locals_, widths, picks):
+        part = received[:, offset:offset + width]
+        offset += width
+        select = (pick[:, None] == jnp.arange(part.shape[0])).astype(part.dtype)
+        chosen = jnp.dot(select, part, preferred_element_type=jnp.float32).astype(part.dtype)
+        results.append(chosen.reshape(pick.shape[0], *local.shape[1:]))
+    return results
 
 
 def on_device(
@@ -178,12 +168,13 @@
     wanted = adapter_row_index[request_adapter]
     down_width = adapter_down_rows.shape[2]
     adapters = jnp.concatenate([adapter_down_rows, adapter_up_query], axis=2)
-    chosen = route(adapters, wanted, "gz", "gx")
+    chosen, cache_keys = route(
+        (adapters, cached_rotated_keys), (wanted, request_cache_block), "gz", "gx"
+    )
+    (cache_values,) = route((cached_value_rows,), (request_cache_block,), "gx", "gz")
     chosen_down = chosen[:, :, :down_width]
     chosen_up = chosen[:, :, down_width:]
-    cache_keys = route(cached_rotated_keys, request_cache_block, "gz", "gx")
-    cache_values = route(cached_value_rows, request_cache_block, "gx", "gz")
-    full_down = gather_model(chosen_down, 2)
+    full_down = lax.all_gather(chosen_down, ("my", "mc"), axis=2, tiled=True)
 
     whole = lax.all_gather(stream, ("my", "mc"), axis=1, tiled=True)
     wide = whole.astype(jnp.float32)
@@ -219,7 +210,8 @@
     values = jnp.dot(normalized_input, value_weight, preferred_element_type=jnp.float32).astype(
         jnp.bfloat16
     )
-    prev_keys, prev_values = shifted((keys, values), ("gx", "gz"), 1)
+    prev_both = shifted(jnp.concatenate([keys, values], axis=1), ("gx", "gz"), 1)
+    prev_keys, prev_values = prev_both[:, : keys.shape[1]], prev_both[:, keys.shape[1]:]
     attended = attend(
         query_vectors,
         keys,

time: 249 us -> 243 us (0.976)
  waiting for transfers between devices: 57.1 us -> 97.4 us
  starting transfers between devices: 44.6 us -> 12.8 us
  local copies, waits for them, and re-layouts: 58.3 us -> 32.4 us
  blocking collectives: 0 us -> 21.5 us
  other arithmetic: 42.4 us -> 27 us
  matrix products: 28.5 us -> 34.8 us
    ppermute x25 -> x0, starting transfers between devices: 38.6 us -> none  [the longest x9 15.8 us: route(): lax.ppermute(payload, second, [(i, (i + step) % SIDE) for i in range(SIDE)])]
    all_gather x0 -> x2, waiting for transfers between devices: none -> 35.4 us  [route(): held_all = lax.all_gather(packed, first, axis=0, tiled=False)]
    all_to_all x0 -> x2, waiting for transfers between devices: none -> 25 us  [route(): lax.all_to_all(jnp.concatenate(payloads, axis=2), second, split_axis=0, c...]
    gather x16 -> x6, local copies, waits for them, and re-layouts: 27 us -> 3.35 us  [route(): source = owner_a[dests] * per_owner + (wanted % per_owner)[dests]]
    all_gather x0 -> x1, blocking collectives: none -> 21.5 us  [on_device(): full_down = lax.all_gather(chosen_down, ('my', 'mc'), axis=2, tiled=True)]
    ppermute x25 -> x0, waiting for transfers between devices: 20.4 us -> none  [the longest x9 15.2 us: route(): lax.ppermute(payload, second, [(i, (i + step) % SIDE) for i in range(SIDE)])]
    another operation x10 -> x3, other arithmetic: 16.2 us -> 2.28 us  [the longest x3 7.18 us: route(): stacked = jnp.stack(received)]
    unnamed x60 -> x47, local copies, waits for them, and re-layouts: 17.5 us -> 3.98 us
  transfers between devices with their start and end apart: 29 -> 7, of which waited for: 6 -> 5; matrix products, arithmetic and copies ran while one was open for 42% -> 28% of each run, Pallas kernels for 0% -> 0%
where the time goes in v2:
time: 243 us; the launch traced here: 242 us
  waiting for transfers between devices  97.4 us (40%)
  matrix products  34.8 us (14%)
  local copies, waits for them, and re-layouts  32.4 us (13%)
  other arithmetic  27 us (11%)
  blocking collectives  21.5 us (9%)
  between operations  15.9 us (7%)
  starting transfers between devices  12.8 us (5%)
    reduce_scatter x1, waiting for transfers between devices, on_device(): lax.psum_scatter(partial_out.astype(jnp.bfloat16), ('my', 'mc'), scatter_...  36.2 us
    all_gather x2, waiting for transfers between devices, route(): held_all = lax.all_gather(packed, first, axis=0, tiled=False)  35.4 us
    all_to_all x2, waiting for transfers between devices, route(): lax.all_to_all(jnp.concatenate(payloads, axis=2), second, split_axis=0, c...  25 us
    all_gather x1, blocking collectives, on_device(): full_down = lax.all_gather(chosen_down, ('my', 'mc'), axis=2, tiled=True)  21.5 us
    all_to_all x2, starting transfers between devices, route(): lax.all_to_all(jnp.concatenate(payloads, axis=2), second, split_axis=0, c...  9.17 us
    all_gather x1, other arithmetic, route(): held_all = lax.all_gather(packed, first, axis=0, tiled=False)  8.13 us
    dot_general x3, matrix products, route(): jnp.dot(select, part, preferred_element_type=jnp.float32).astype(part.dtype)  6.35 us
    dot_general x1, matrix products, on_device(): jnp.dot(low * own_columns, chosen_up.reshape(REQS * rank_index, -1), pref...  6.25 us
  transfers between devices with their start and end apart: 7, of which 5 were waited for; matrix products, arithmetic and copies ran while one was open for 28% of the time, Pallas kernels for 0%

profile of v2, /device:TPU:0, one launch (start us, length us, event | category | flops | bytes accessed | tf_op | source)
XLA Modules:
  0.0 241.8 jit_solution(16727356542782356125)
XLA Ops:
  6.5 2.0 reshape.477
  8.6 1.0 pad_maximum_fusion.3
  9.8 1.2 copy.92
  10.9 0.8 pad_maximum_fusion.2
  11.8 0.7 all-gather.6.cloned.1.call-update
  12.8 0.8 gather_fusion.2
  13.7 0.6 constant_dynamic-slice_fusion.8
  14.9 0.6 dynamic_slice.24
  17.6 0.5 fusion.108
  18.1 2.2 compare_select_fusion.2
  20.7 0.6 gather_fusion.5
  21.3 0.6 gather_fusion.4
  21.8 0.6 gather_fusion.6
  22.4 0.6 gather_fusion.1
  22.9 0.6 gather_fusion
  23.5 0.6 gather_fusion.3
  24.1 18.2 %all-gather.10.cloned.1.call-done = bf16[4,1,131072]{2,1,0:T(2,128)(2,1)} async-done(((bf16[1,1,131072]{2,1,0:T(2,128)(2,1)}), bf16[4,1,131072]{2,1,0:T(2,128)(2,1)}) %all-gather.10.cloned.1.call-update) | async-done | bytes 1048592 | tf_op jit(solution)/shard_map/all_gather | solution.py:113
  42.3 8.1 %reduce.2 = bf16[4,131072]{1,0:T(4,128)(2,1)S(1)} reduce(bf16[4,1,131072]{2,1,0:T(2,128)(2,1)} %all-gather.10.cloned.1.call-done, bf16[]{:T(256)} %constant.173), dimensions={1}, to_apply=%all-gather.1.reduce_sub_computation | reduce | bytes 2097154 | tf_op jit(solution)/shard_map/all_gather | solution.py:113
  50.5 1.3 reshape.483
  51.8 3.4 %convolution_convert_fusion.1 = bf16[4,4,65536]{2,1,0:T(4,128)(2,1)} fusion(bf16[8,65536,1]{1,0,2:T(8,128)(2,1)} %reshape.483, s32[4,4]{1,0:T(4,128)S(1)} %multiply_add_fusion.2), kind=kOutput, calls=%fused_computation.8 | convolution fusion | flops 17825920 | bytes 3145792 | tf_op jit(solution)/shard_map/dsj,jn->dsn/dot_general | solution.py:127
  55.2 4.6 %all-to-all-start = ((bf16[4,4,65536]{2,1,0:T(4,128)(2,1)}), bf16[4,4,65536]{2,1,0:T(4,128)(2,1)}, u32[]{:S(2)}, u32[]{:S(2)}) async-start(bf16[4,4,65536]{2,1,0:T(4,128)(2,1)} %convolution_convert_fusion.1), calls=%async_computation | async-start | bytes 4194304 | tf_op jit(solution)/shard_map/all_to_all | solution.py:134
  59.8 17.2 %all-gather.8.cloned.1.call-done = bf16[770048]{0:T(1024)(128)(2,1)} async-done(((bf16[192512]{0:T(1024)(128)(2,1)}), bf16[770048]{0:T(1024)(128)(2,1)}) %all-gather.8.cloned.1.call-update) | async-done | bytes 1540112 | tf_op jit(solution)/shard_map/all_gather | solution.py:113
  77.0 2.0 reshape.451
  79.0 1.0 slice.75
  80.0 1.4 slice.76
  81.3 1.5 reshape.485
  82.8 1.3 reshape.484
  84.2 0.4 convolution_convert_fusion.4
  84.5 0.8 convolution_convert_fusion
  85.3 2.7 %pad_maximum_fusion = bf16[4,4,80896]{2,1,0:T(4,128)(2,1)} fusion(bf16[4,4,65536]{2,1,0:T(4,128)(2,1)S(1)} %convolution_convert_fusion, bf16[4,4,15360]{2,1,0:T(4,128)(2,1)S(1)} %convolution_convert_fusion.4), kind=kLoop, calls=%fused_computation.31 | loop fusion | flops 5177344 | bytes 5177344 | tf_op jit(solution)/shard_map/concatenate | solution.py:135
  88.0 5.0 %all-to-all-done = bf16[4,4,65536]{2,1,0:T(4,128)(2,1)} async-done(((bf16[4,4,65536]{2,1,0:T(4,128)(2,1)}), bf16[4,4,65536]{2,1,0:T(4,128)(2,1)}, u32[]{:S(2)}, u32[]{:S(2)}) %all-to-all-start) | async-done | bytes 2097184 | tf_op jit(solution)/shard_map/all_to_all | solution.py:134
  92.9 4.5 %all-to-all-start.1 = ((bf16[4,4,80896]{2,1,0:T(4,128)(2,1)}), bf16[4,4,80896]{2,1,0:T(4,128)(2,1)}, u32[]{:S(2)}, u32[]{:S(2)}) async-start(bf16[4,4,80896]{2,1,0:T(4,128)(2,1)} %pad_maximum_fusion), calls=%async_computation.1 | async-start | bytes 5177344 | tf_op jit(solution)/shard_map/all_to_all | solution.py:134
  97.7 0.2 fusion.42
  97.9 1.8 multiply_cosine_fusion
  99.8 0.8 compare_and_fusion
  100.6 0.4 pad_add_fusion
  100.9 2.9 %reshape.374 = bf16[16,65536]{1,0:T(8,128)(2,1)} reshape(bf16[4,4,65536]{2,1,0:T(4,128)(2,1)} %all-to-all-done) | data formatting | bytes 4194304 | tf_op jit(solution)/shard_map/reshape | solution.py:137
  103.9 3.0 %convolution_convert_fusion.3 = bf16[4,65536]{1,0:T(4,128)(2,1)} fusion(bf16[16,65536]{1,0:T(8,128)(2,1)} %reshape.374, s32[4]{0:T(128)S(1)} %fusion.86), kind=kOutput, calls=%fused_computation.10 | convolution fusion | flops 8650816 | bytes 2621456 | tf_op jit(solution)/shard_map/dot_general | solution.py:143
  106.8 1.5 reshape_reshape.12
  108.3 1.0 copy.73
  109.3 20.0 %all-to-all-done.1 = bf16[4,4,80896]{2,1,0:T(4,128)(2,1)} async-done(((bf16[4,4,80896]{2,1,0:T(4,128)(2,1)}), bf16[4,4,80896]{2,1,0:T(4,128)(2,1)}, u32[]{:S(2)}, u32[]{:S(2)}) %all-to-all-start.1) | async-done | bytes 2588704 | tf_op jit(solution)/shard_map/all_to_all | solution.py:134
  129.3 3.2 %reshape.380 = bf16[16,80896]{1,0:T(8,128)(2,1)} reshape(bf16[4,4,80896]{2,1,0:T(4,128)(2,1)} %all-to-all-done.1) | data formatting | bytes 5177344 | tf_op jit(solution)/shard_map/reshape | solution.py:137
  132.5 2.1 convolution_convert_fusion.2
  134.6 1.2 reshape_reshape.15
  135.8 1.3 convolution_convert_fusion.5
  137.3 0.3 copy.79
  137.6 21.5 %all_gather.19 = bf16[4,16,3584]{1,0,2:T(4,128)(2,1)} all-gather(bf16[4,16,448]{1,0,2:T(4,128)(2,1)S(1)} %copy.79), channel_id=1, replica_groups=mesh['gx'=4,'gz'=4,'my'=4,'mc'=2] {'my','mc'}, dimensions={2}, use_global_device_ids=true | all-gather | bytes 516096 | tf_op jit(solution)/shard_map/all_gather | solution.py:177
  159.1 3.0 %fusion.2 = f32[512]{0:T(512)S(1)} fusion(bf16[512,3584]{0,1:T(8,128)(2,1)} %all-gather.6.cloned.1.call-done), kind=kLoop, calls=%fused_computation.19 | loop fusion | flops 5504512 | bytes 3672064 | tf_op jit(solution)/shard_map/reduce_sum | solution.py:182
  162.2 1.5 convolution_bitcast_fusion.1
  163.7 1.2 fusion.54
  164.9 0.8 copy.78
  165.8 4.2 %convolution_convert_fusion.7 = bf16[512,256]{0,1:T(8,128)(2,1)S(1)} fusion(bf16[3584,256]{1,0:T(8,128)(2,1)} %param.20, bf16[512,3584]{0,1:T(8,128)(2,1)} %all-gather.6.cloned.1.call-done, f32[3584]{0:T(1024)S(1)} %copy-done.18, f32[512]{0:T(512)S(1)} %add_rsqrt_fusion), kind=kOutput, calls=%fused_computation.39 | convolution fusion | flops 946995200 | bytes 5783552 | tf_op jit(solution)/shard_map/dot_general | solution.py:210
  170.0 0.9 pad_maximum_fusion.1
  170.9 3.5 %collective-permute-start = (bf16[512,512]{0,1:T(8,128)(2,1)}, bf16[512,512]{0,1:T(8,128)(2,1)}, u32[]{:S(2)}, u32[]{:S(2)}) collective-permute-start(bf16[512,512]{0,1:T(8,128)(2,1)} %pad_maximum_fusion.1), channel_id=1, source_target_pairs={{0,8},{8,16},{16,24},{24,32},{32,40},{40,48},{48,56},{56,64},{64,7... | collective-permute-start | bytes 1572872 | tf_op jit(solution)/shard_map/ppermute | solution.py:16
  174.4 2.5 %fusion.101 = f32[512,512]{0,1:T(8,128)S(1)} fusion(bf16[3584,512]{1,0:T(8,128)(2,1)S(1)} %copy-done.16, bf16[512,3584]{0,1:T(8,128)(2,1)S(1)} %copy-done.4, f32[3584]{0:T(1024)S(1)} %copy-done.18, f32[512]{0:T(512)S(1)} %add_rsqrt_fusion), kind=kOutput, calls=%fused_computation.193 | convolution fusion | flops 1886388224 | bytes 8404992 | tf_op jit(solution)/shard_map/dot_general | solution.py:201
  176.9 6.2 %fusion.18 = f32[512,512]{0,1:T(8,128)} fusion(f32[512,512]{0,1:T(8,128)S(1)} %fusion.101, bf16[4,16,3584]{1,0,2:T(4,128)(2,1)} %all_gather.19, bf16[4,16,960]{2,1,0:T(8,128)(2,1)S(1)} %reshape.381, bf16[512,4]{0,1:T(4,128)(2,1)S(1)} %convert_convert_fusion, bf16[512,3584]{0,1:T(8,128)(2,1)} %all-gather.6.cloned.1.call-done, f32[3584]{0:T(1024)S(1)} %copy-done.18, ...), kind=kOutput, calls=%fused_computation.37 | convolution fusion | flops 276365312 | bytes 6313984 | tf_op jit(solution)/shard_map/dot_general | solution.py:195
  183.2 1.3 fusion.106
  185.0 0.9 subtract_convert_fusion
  185.9 1.1 fusion.107
  187.1 2.8 %fusion.5 = (f32[2,512]{1,0:T(2,128)S(1)}, f32[2048,512,2]{1,0,2:T(8,128)S(1)}) fusion(pred[512,2048]{0,1:T(8,128)(4,1)S(1)} %pad_add_fusion, bf16[512,2,128]{2,0,1:T(8,128)(2,1)} %get-tuple-element.16, bf16[512,2,128]{2,0,1:T(8,128)(2,1)} %get-tuple-element.15, bf16[512,256]{1,0:T(8,128)(2,1)S(1)} %copy-done.9, bf16[512,256]{1,0:T(8,128)(2,1)S(1)} %copy.77, ...), kind=kOutput, calls=%fused_computation.22 | convolution fusion | flops 1084226560 | bytes 11014144 | tf_op jit(solution)/shard_map/tkrd,skd->krts/dot_general | solution.py:84
  190.0 2.2 fusion
  192.3 2.8 %divide_convert_fusion = bf16[512,1,2,256]{0,3,2,1:T(8,128)(2,1)S(1)} fusion(f32[2048,512,2]{1,0,2:T(8,128)S(1)} %get-tuple-element.35, f32[2,512]{1,0:T(2,128)S(1)} %get-tuple-element.34, pred[512,2048]{0,1:T(8,128)(4,1)S(1)} %pad_add_fusion, bf16[512,256]{0,1:T(8,128)(2,1)S(1)} %copy-done.11, bf16[512,256]{0,1:T(8,128)(2,1)S(1)} %get-tuple-element.21, ...), kind=kOutput, calls=%fused_computation.53 | convolution fusion | flops 1085800448 | bytes 11018240 | tf_op jit(solution)/shard_map/krts,skd->tkrd/dot_general | solution.py:91
  195.1 3.9 %convolution_convert_fusion.6 = bf16[512,3584]{0,1:T(8,128)(2,1)} fusion(bf16[512,512]{0,1:T(8,128)(2,1)S(1)} %bitcast.114, bf16[512,3584]{1,0:T(8,128)(2,1)S(1)} %copy-done.17), kind=kOutput, calls=%fused_computation.23 | convolution fusion | flops 1880883200 | bytes 7864320 | tf_op jit(solution)/shard_map/dot_general | solution.py:229
  199.0 36.2 %reduce-scatter.2.cloned.1.call-done = bf16[512,448]{0,1:T(8,128)(2,1)} async-done(((bf16[512,3584]{0,1:T(8,128)(2,1)}), bf16[512,448]{0,1:T(8,128)(2,1)}) %reduce-scatter.2.cloned.1.call-update) | async-done | bytes 458768 | tf_op jit(solution)/shard_map/reduce_scatter | solution.py:230
  (88 shorter events, 2.6 us)
Async XLA Ops:
  6.5 155.6 %copy-start = (bf16[3584,256]{1,0:T(8,128)(2,1)S(1)}, bf16[3584,256]{1,0:T(8,128)(2,1)}, u32[]{:S(2)}) copy-start(bf16[3584,256]{1,0:T(8,128)(2,1)} %param.19) | copy-start | bytes 5505028
  6.5 6.0 %copy-start.12 = (s32[16,4]{0,1:T(4,128)S(1)}, s32[16,4]{0,1:T(4,128)}, u32[]{:S(2)}) copy-start(s32[16,4]{0,1:T(4,128)} %param.24) | copy-start | bytes 772
  6.5 6.2 %copy-start.2 = (s32[64]{0:T(128)S(1)}, s32[64]{0:T(128)}, u32[]{:S(2)}) copy-start(s32[64]{0:T(128)} %param.25) | copy-start | bytes 772
  6.5 35.8 %all-gather.10.cloned.1.call-start = ((), (), s32[]{:S(2)}) async-start(), calls=%async_computation.6 | async-start | bytes 2621440 | tf_op jit(solution)/shard_map/all_gather | solution.py:113
  8.6 68.5 %all-gather.8.cloned.1.call-start = ((), (), s32[]{:S(2)}) async-start(), calls=%async_computation.5 | async-start | bytes 1925120 | tf_op jit(solution)/shard_map/all_gather | solution.py:113
  11.7 147.4 %all-gather.6.cloned.1.call-start = ((), (), s32[]{:S(2)}) async-start(), calls=%async_computation.3 | async-start | bytes 4128768 | tf_op jit(solution)/shard_map/all_gather | solution.py:179
  12.7 1.0 copy-start.15
  12.7 2.1 copy-start.19
  12.7 4.4 %copy-start.14 = (s32[16,4]{0,1:T(4,128)S(1)}, s32[16,4]{0,1:T(4,128)}, u32[]{:S(2)}) copy-start(s32[16,4]{0,1:T(4,128)} %param.29) | copy-start | bytes 772
  12.8 7.8 %copy-start.13 = (s32[16,4]{0,1:T(4,128)S(1)}, s32[16,4]{0,1:T(4,128)}, u32[]{:S(2)}) copy-start(s32[16,4]{0,1:T(4,128)} %param.28) | copy-start | bytes 772
  55.2 37.8 %all-to-all-start = ((bf16[4,4,65536]{2,1,0:T(4,128)(2,1)}), bf16[4,4,65536]{2,1,0:T(4,128)(2,1)}, u32[]{:S(2)}, u32[]{:S(2)}) async-start(bf16[4,4,65536]{2,1,0:T(4,128)(2,1)} %convolution_convert_fusion.1), calls=%async_computation | async-start | bytes 4194304 | tf_op jit(solution)/shard_map/all_to_all | solution.py:134
  92.9 36.4 %all-to-all-start.1 = ((bf16[4,4,80896]{2,1,0:T(4,128)(2,1)}), bf16[4,4,80896]{2,1,0:T(4,128)(2,1)}, u32[]{:S(2)}, u32[]{:S(2)}) async-start(bf16[4,4,80896]{2,1,0:T(4,128)(2,1)} %pad_maximum_fusion), calls=%async_computation.1 | async-start | bytes 5177344 | tf_op jit(solution)/shard_map/all_to_all | solution.py:134
  97.5 137.8 %reduce-scatter.2.cloned.1.call-start = ((), (), s32[]{:S(2)}) async-start(), calls=%async_computation.4 | async-start | bytes 4128768 | tf_op jit(solution)/shard_map/reduce_scatter | solution.py:230
  137.6 24.6 %copy-start.18 = (f32[3584]{0:T(1024)S(1)}, f32[3584]{0:T(1024)}, u32[]{:S(2)}) copy-start(f32[3584]{0:T(1024)} %param.17) | copy-start | bytes 43012
  159.1 3.1 %copy-start.3 = (bf16[512,3584]{0,1:T(8,128)(2,1)S(1)}, bf16[512,3584]{0,1:T(8,128)(2,1)}, u32[]{:S(2)}) copy-start(bf16[512,3584]{0,1:T(8,128)(2,1)} %all-gather.6.cloned.1.call-done) | copy-start | bytes 11010052
  165.8 8.7 %copy-start.4 = (bf16[512,3584]{0,1:T(8,128)(2,1)S(1)}, bf16[512,3584]{0,1:T(8,128)(2,1)}, u32[]{:S(2)}) copy-start(bf16[512,3584]{0,1:T(8,128)(2,1)} %all-gather.6.cloned.1.call-done) | copy-start | bytes 11010052
  165.8 8.7 %copy-start.16 = (bf16[3584,512]{1,0:T(8,128)(2,1)S(1)}, bf16[3584,512]{1,0:T(8,128)(2,1)}, u32[]{:S(2)}) copy-start(bf16[3584,512]{1,0:T(8,128)(2,1)} %param.18) | copy-start | bytes 11010052
  170.0 7.0 %copy-start.10 = (bf16[512,256]{0,1:T(8,128)(2,1)}, bf16[512,256]{0,1:T(8,128)(2,1)S(1)}, u32[]{:S(2)}) copy-start(bf16[512,256]{0,1:T(8,128)(2,1)S(1)} %convolution_convert_fusion.7) | copy-start | bytes 786436
  170.9 15.0 %collective-permute-start = (bf16[512,512]{0,1:T(8,128)(2,1)}, bf16[512,512]{0,1:T(8,128)(2,1)}, u32[]{:S(2)}, u32[]{:S(2)}) collective-permute-start(bf16[512,512]{0,1:T(8,128)(2,1)} %pad_maximum_fusion.1), channel_id=1, source_target_pairs={{0,8},{8,16},{16,24},{24,32},{32,40},{40,48},{48,56},{56,64},{64,7... | collective-permute-start | bytes 1572872 | tf_op jit(solution)/shard_map/ppermute | solution.py:16
  183.2 1.8 copy-start.5
  183.2 1.8 copy-start.6
  183.2 3.9 %copy-start.9 = (bf16[512,256]{1,0:T(8,128)(2,1)S(1)}, bf16[512,256]{1,0:T(8,128)(2,1)}, u32[]{:S(2)}) copy-start(bf16[512,256]{1,0:T(8,128)(2,1)} %copy.78) | copy-start | bytes 786436
  184.9 2.2 copy-start.8
  190.0 2.3 copy-start.7
  190.0 2.3 copy-start.11
  192.3 2.8 %copy-start.17 = (bf16[512,3584]{1,0:T(8,128)(2,1)S(1)}, bf16[512,3584]{1,0:T(8,128)(2,1)}, u32[]{:S(2)}) copy-start(bf16[512,3584]{1,0:T(8,128)(2,1)} %param.21) | copy-start | bytes 11010052
  195.1 40.2 %copy-start.1 = (bf16[3584,256]{1,0:T(8,128)(2,1)S(1)}, bf16[3584,256]{1,0:T(8,128)(2,1)}, u32[]{:S(2)}) copy-start(bf16[3584,256]{1,0:T(8,128)(2,1)} %param.19) | copy-start | bytes 5505028
Sparse Core Ops, SparseCore 0:
  9.0 33.2 all-gather.9
  44.0 32.9 all-gather.7
  78.7 31.4 all-gather.5
  199.1 36.0 reduce-scatter.1
